TPU v7x, 32 devices: a whole 2x2x4 slice. The times are simulated.
32 devices in a mesh: groups: 2 (over x), tm: 16 (over z, y, core).
Axes of the slice: x: 2, y: 2, z: 4, core: 2. Of those that a mesh axis runs over, the one named last changes fastest.
Arguments:
- hyper: float32 [6], P('groups'), parts along dimension 0, may hold values from 0.5 to 0.9
- spatial_prec: float32 [768, 768], replicated, as said below
- part_lengths: int32 [32], P('groups'), parts along dimension 0, may hold values from 1 to 2, as said below
- reading_index: int32 [4, 32, 1024], P(None, ('groups', 'tm')), parts along dimension 1, may hold values from 0 to 767, as said below
- reading_value: float32 [4, 32, 1024], P(None, ('groups', 'tm')), parts along dimension 1, as said below
- reading_cov: float32 [16, 32, 1024], P(None, ('groups', 'tm')), parts along dimension 1, may hold values from -0.1875 to 0.1875
Outputs:
- sep_block: float32 [32, 768, 768], P(('groups', 'tm')), parts along dimension 0
- fill_block: float32 [32, 768, 768], P(('groups', 'tm')), parts along dimension 0
- sep_border: float32 [32, 16, 768], P(('groups', 'tm')), parts along dimension 0
- tip: float32 [32, 16], P('groups'), parts along dimension 0
There are 2 independent parts, one for each index of `groups`. A program takes and returns all parts, laid end to end along the dimension named above; an argument that names none is the same for every part. Nothing has to cross between parts.
Inputs may be any that keep to these rules, and one draw needn't show every extreme that they name: `reading_index`: row 0 is a reading's day, rows 1 to 3 the mesh nodes of its triangle's vertices. On every device, column block k (columns k * 64 to (k + 1) * 64 - 1) holds readings whose day lies in time partition k. `part_lengths`: partition k holds the days that follow those of partitions 0 to k - 1; exactly 8 partitions hold 2 days, the others 1. `reading_value`: row 0 is the linear predictor; rows 1 to 3 are positive barycentric weights summing to 1 for each reading. `spatial_prec`: A symmetric sparse mesh precision: each row has a few nonpositive neighbour entries, and a positive diagonal that exceeds the sum of magnitudes of its row's other entries.
All inputs are finite; a program needn't handle non-finite values.
Results may differ from a plain program's by a relative error of at most 0.0003.
Values sent between devices are 32-bit elements; how exact they have to be, the bound alone decides.
No kernel may reach another device: no remote copies, remote signals or barrier semaphores. Data moves between devices by JAX's collectives and lax.ppermute only.
A program may use at most 128 MiB of HBM per device.

v0:
```python
import jax
import jax.numpy as jnp
from jax import lax
from jax.sharding import PartitionSpec as P
from jax.experimental import pallas as pl
from jax.experimental.pallas import tpu as pltpu

HIGHEST = lax.Precision.HIGHEST


def passed_along(x, axis, by):
    length = lax.axis_size(axis)
    pairs = [(i, i + by) for i in range(length) if 0 <= i + by < length]
    return lax.ppermute(x, axis, pairs)


def matmul_high(left, right):
    return jnp.dot(left, right, precision=HIGHEST)


def contract_rows(left, right):
    return lax.dot_general(
        left, right, (((0,), (0,)), ((), ())), preferred_element_type=jnp.float32
    )


def split_dot(left, right):
    dims = (((1,), (1,)), ((), ()))
    left_hi = left.astype(jnp.bfloat16)
    left_lo = (left - left_hi.astype(jnp.float32)).astype(jnp.bfloat16)
    right_hi = right.astype(jnp.bfloat16)
    right_lo = (right - right_hi.astype(jnp.float32)).astype(jnp.bfloat16)
    out = lax.dot_general(left_hi, right_hi, dims, preferred_element_type=jnp.float32)
    out = out + lax.dot_general(left_hi, right_lo, dims, preferred_element_type=jnp.float32)
    out = out + lax.dot_general(left_lo, right_hi, dims, preferred_element_type=jnp.float32)
    return out


def assemble_kernel(end_ref, packed_ref, hessian_ref, border_ref, tip_ref):
    mesh_width = hessian_ref.shape[1]
    covars = border_ref.shape[1]

    @pl.when(pl.program_id(0) == 0)
    def _():
        hessian_ref[...] = jnp.zeros_like(hessian_ref)
        border_ref[...] = jnp.zeros_like(border_ref)
        tip_ref[...] = jnp.zeros_like(tip_ref)

    chunk = packed_ref.shape[1]
    my_end = end_ref[0]
    day = packed_ref[0:1, :]
    weight = jnp.exp(packed_ref[4:5, :])
    nodes = lax.broadcasted_iota(jnp.int32, (mesh_width, chunk), 0).astype(jnp.float32)
    incidence = jnp.zeros((mesh_width, chunk), jnp.float32)
    for u in range(3):
        incidence = incidence + jnp.where(
            nodes == packed_ref[1 + u : 2 + u, :], packed_ref[5 + u : 6 + u, :], 0.0
        )
    covariate = packed_ref[8 : 8 + covars, :]
    for slot in range(2):
        chosen = jnp.where(day == my_end - slot, weight, 0.0)
        weighted = incidence * chosen
        hessian_ref[slot] += split_dot(incidence, weighted)
        border_ref[slot] += split_dot(covariate, weighted)
    tip_ref[...] += split_dot(covariate * weight, covariate)


def assemble(packed, my_end, mesh_width, covars):
    total_reads = packed.shape[1] * packed.shape[2]
    rows = packed.shape[0]
    packed = packed.reshape(rows, total_reads)
    chunk = 512 if total_reads % 512 == 0 else total_reads
    end_value = my_end.astype(jnp.float32).reshape(1)
    hessian, border, tip_data = pl.pallas_call(
        assemble_kernel,
        grid=(total_reads // chunk,),
        in_specs=[
            pl.BlockSpec(memory_space=pltpu.SMEM),
            pl.BlockSpec((rows, chunk), lambda i: (0, i)),
        ],
        out_specs=[
            pl.BlockSpec((2, mesh_width, mesh_width), lambda i: (0, 0, 0)),
            pl.BlockSpec((2, covars, mesh_width), lambda i: (0, 0, 0)),
            pl.BlockSpec((covars, covars), lambda i: (0, 0)),
        ],
        out_shape=[
            jax.ShapeDtypeStruct((2, mesh_width, mesh_width), jnp.float32),
            jax.ShapeDtypeStruct((2, covars, mesh_width), jnp.float32),
            jax.ShapeDtypeStruct((covars, covars), jnp.float32),
        ],
        compiler_params=pltpu.CompilerParams(
            dimension_semantics=("arbitrary",), vmem_limit_bytes=48 * 1024 * 1024
        ),
    )(end_value, packed)
    return (hessian, border, tip_data)


def split_parts(value):
    high = value.astype(jnp.bfloat16)
    low = (value - high.astype(jnp.float32)).astype(jnp.bfloat16)
    return high, low


def split_matmul(left, right):
    left_hi, left_lo = split_parts(left)
    right_hi, right_lo = split_parts(right)
    out = jnp.dot(left_hi, right_hi, preferred_element_type=jnp.float32)
    out = out + jnp.dot(left_hi, right_lo, preferred_element_type=jnp.float32)
    out = out + jnp.dot(left_lo, right_hi, preferred_element_type=jnp.float32)
    return out


def exact_matmul(left, right):
    return jnp.dot(left, right, precision=HIGHEST, preferred_element_type=jnp.float32)


def sweep(block_ref):
    size = block_ref.shape[0]
    lane = lax.broadcasted_iota(jnp.int32, (size, size), 1)
    sub = lax.broadcasted_iota(jnp.int32, (size, size), 0)
    lane_row = lax.broadcasted_iota(jnp.int32, (1, size), 1)

    def body(k, carry):
        current = block_ref[...]
        row = block_ref[pl.ds(k, 1), :]
        col = jnp.sum(jnp.where(lane == k, current, 0.0), axis=1, keepdims=True)
        pivot = jnp.sum(jnp.where(lane_row == k, row, 0.0), axis=1, keepdims=True)
        inverse = 1.0 / pivot
        scaled_row = row * inverse
        update = current - col * scaled_row
        update = jnp.where(sub == k, scaled_row, update)
        update = jnp.where(lane == k, col * inverse, update)
        update = jnp.where((sub == k) & (lane == k), -inverse, update)
        block_ref[...] = update
        return carry

    lax.fori_loop(0, size, body, 0)


def eliminate_kernel(start_ref, work_ref, solved_ref, block_ref):
    mesh_width = work_ref.shape[0]
    block_size = block_ref.shape[0]
    work_ref[...] = start_ref[...]
    for col in range(mesh_width // block_size):
        lo = col * block_size
        hi = lo + block_size
        block_ref[...] = work_ref[lo:hi, lo:hi]
        sweep(block_ref)
        solved = -exact_matmul(block_ref[...], work_ref[lo:hi, hi:])
        solved_ref[lo:hi, :] = solved[:, mesh_width - hi :]
        if hi < mesh_width:
            work_ref[hi:, hi:] = work_ref[hi:, hi:] - exact_matmul(work_ref[hi:, lo:hi], solved)


def eliminate(hessian, border, prior_diag, coupling_block):
    mesh_width = coupling_block.shape[0]
    block_size = 128 if mesh_width % 128 == 0 else mesh_width
    interior = hessian[1] + prior_diag
    start = jnp.concatenate([interior, coupling_block, border[1].T], axis=1)
    width = start.shape[1]
    work, solved = pl.pallas_call(
        eliminate_kernel,
        out_shape=[
            jax.ShapeDtypeStruct((mesh_width, width), jnp.float32),
            jax.ShapeDtypeStruct((mesh_width, width - mesh_width), jnp.float32),
        ],
        in_specs=[pl.BlockSpec(memory_space=pltpu.VMEM)],
        out_specs=[pl.BlockSpec(memory_space=pltpu.VMEM), pl.BlockSpec(memory_space=pltpu.VMEM)],
        scratch_shapes=[pltpu.VMEM((block_size, block_size), jnp.float32)],
        compiler_params=pltpu.CompilerParams(vmem_limit_bytes=60 * 1024 * 1024),
    )(start)
    schur = -lax.dot_general(
        work[:, mesh_width:], solved, (((0,), (0,)), ((), ())), precision=HIGHEST
    )
    schur_update = schur[:mesh_width, :mesh_width]
    lateral_block = schur[mesh_width:, :mesh_width]
    apex_schur_block = schur[mesh_width:, mesh_width:]
    return (schur_update, lateral_block, apex_schur_block)


def local(hyper, spatial_prec, part_lengths, reading_index, reading_value, reading_cov):
    packed = jnp.concatenate(
        [reading_index.astype(jnp.float32), reading_value, reading_cov], axis=0
    )
    packed = lax.all_to_all(packed, "tm", split_axis=2, concat_axis=1, tiled=True)
    mesh_width = spatial_prec.shape[0]
    covars = reading_cov.shape[0]
    partition_position = lax.axis_index("tm")
    corr_time = hyper[0]
    tau_field = hyper[1]
    tau_fixed = hyper[2]
    prior_diag = (1.0 + corr_time * corr_time) * tau_field * spatial_prec
    coupling_block = -corr_time * tau_field * spatial_prec
    part_ends = (jnp.cumsum(part_lengths) - 1).astype(jnp.int32)
    my_end = part_ends[partition_position]
    local_length = part_lengths[partition_position]
    hessian, border, tip_data = assemble(packed, my_end, mesh_width, covars)

    def bypass_elimination():
        return (
            jnp.zeros_like(coupling_block),
            jnp.zeros((covars, mesh_width), coupling_block.dtype),
            jnp.zeros((covars, covars), coupling_block.dtype),
        )

    def perform_elimination():
        return eliminate(hessian, border, prior_diag, coupling_block)

    schur_update, lateral_block, apex_schur_block = lax.cond(
        local_length == 2, perform_elimination, bypass_elimination
    )
    has_left = partition_position > 0
    fill = jnp.where(has_left, jnp.where(local_length == 2, schur_update, coupling_block), 0.0)
    left_update = jnp.where(has_left, schur_update, 0.0)
    left_side = jnp.where(has_left, lateral_block, 0.0)
    from_right, from_right_side = passed_along((left_update, left_side), "tm", -1)
    sep_block = hessian[0] + prior_diag + schur_update + from_right
    sep_border = border[0] + lateral_block + from_right_side
    tip_total = lax.psum(tip_data + apex_schur_block, "tm")
    tip = tip_total + tau_fixed * jnp.eye(covars, dtype=jnp.float32)
    return (sep_block[None], fill[None], sep_border[None], tip)


def solution(mesh):
    in_specs = (
        P("groups"),
        P(),
        P("groups"),
        P(None, ("groups", "tm"), None),
        P(None, ("groups", "tm"), None),
        P(None, ("groups", "tm"), None),
    )
    out_specs = (
        P(("groups", "tm"), None, None),
        P(("groups", "tm"), None, None),
        P(("groups", "tm"), None, None),
        P("groups", None),
    )
    return jax.shard_map(local, mesh=mesh, in_specs=in_specs, out_specs=out_specs, check_vma=False)
```

profile of v0, /device:TPU:0, one launch (start us, length us, event | category | flops | bytes accessed | tf_op | source)
XLA Modules:
  0.0 225.3 jit_solution(14096496929827076113)
XLA Ops:
  0.6 0.7 convert_element_type.16
  1.4 0.3 copy.29
  1.7 1.0 copy.30
  2.7 0.0 copy-start
  2.7 1.0 copy.31
  3.8 2.2 fusion.12
  6.0 0.5 broadcast.22
  6.6 1.9 reduce
  8.5 1.0 reshape.57
  9.5 7.4 %all-to-all-start = ((f32[16,1,1536]{2,1,0:T(1,128)}), f32[16,1,1536]{2,1,0:T(1,128)S(1)}, u32[]{:S(2)}, u32[]{:S(2)}) async-start(f32[16,1,1536]{2,1,0:T(1,128)} %reshape.57), calls=%async_computation | async-start | bytes 196608 | tf_op jit(solution)/shard_map/all_to_all | solution.py:185
  16.9 0.6 fusion.10
  20.8 0.0 copy-start.1
  20.8 3.4 %broadcast_multiply_fusion = (f32[768,768]{1,0:T(8,128)S(1)}, f32[768,768]{1,0:T(8,128)}) fusion(f32[768,768]{1,0:T(8,128)} %param.9, f32[]{:T(128)} %bitcast.9, f32[]{:T(128)} %bitcast.7), kind=kLoop, calls=%fused_computation.12 | loop fusion | flops 1179648 | bytes 7077896 | tf_op jit(solution)/shard_map/mul | solution.py:193
  24.2 0.6 dynamic_slice.7
  25.4 0.1 copy.28
  25.5 0.6 fusion.11
  26.8 0.0 all-to-all-done
  26.8 0.9 reduce.1
  27.7 0.9 reshape.58
  28.6 0.3 copy.32
  28.9 13.4 %shard_map.93 = (f32[2,768,768]{2,1,0:T(8,128)}, f32[2,16,768]{2,1,0:T(8,128)S(1)}, f32[16,16]{1,0:T(8,128)S(1)}) custom-call(f32[1]{0:T(128)} %bitcast.4.end_ref, f32[24,1024]{1,0:T(8,128)S(1)} %bitcast.38), custom_call_target="tpu_custom_call" | custom-call | tf_op jit(solution)/shard_map/pallas_call | solution.py:74
  42.3 1.6 conditional.1
  42.3 1.6 broadcast.13
  43.8 4.2 %select_bitcast_fusion = (f32[1,768,768]{2,1,0:T(8,128)}, f32[768,768]{1,0:T(8,128)}) fusion(f32[768,768]{1,0:T(8,128)} %get-tuple-element.26, f32[768,768]{1,0:T(8,128)S(1)} %get-tuple-element.48, pred[]{:T(512)} %bitcast.8, pred[]{:T(512)S(6)} %gt.3), kind=kLoop, calls=%fused_computation.10 | loop fusion | flops 1769472 | bytes 9437186 | tf_op jit(solution)/shard_map/broadcast_in_dim | solution.py:221
  48.0 1.3 collective-permute-start
  49.3 1.3 collective-permute-start.1
  50.6 167.7 %psum.7 = f32[16,16]{1,0:T(8,128)S(1)} all-reduce(f32[16,16]{1,0:T(8,128)S(1)} %add.38), channel_id=1, replica_groups=mesh['groups'=2,'tm'=16] {'tm'}, use_global_device_ids=true, to_apply=%region_3.4 | all-reduce | flops 256 | bytes 2048 | tf_op jit(solution)/shard_map/psum | solution.py:219
  218.3 1.2 select_add_fusion
  219.6 0.0 collective-permute-done.1
  219.6 0.6 fusion.9
  220.2 0.0 collective-permute-done
  220.2 5.1 %fusion.7 = f32[1,768,768]{2,1,0:T(8,128)} fusion(f32[768,768]{1,0:T(8,128)S(1)} %collective-permute-done, f32[768,768]{1,0:T(8,128)} %get-tuple-element.26, f32[768,768]{1,0:T(8,128)} %get-tuple-element.49, f32[2,768,768]{2,1,0:T(8,128)} %get-tuple-element.24), kind=kLoop, calls=%fused_computation.9 | loop fusion | flops 1769472 | bytes 11796480 | tf_op jit(solution)/shard_map/broadcast_in_dim | solution.py:221
  (7 shorter events, 0.1 us)
Async XLA Ops:
  2.7 14.2 %copy-start = (f32[3]{0:T(128)S(1)}, f32[3]{0:T(128)}, u32[]{:S(2)}) copy-start(f32[3]{0:T(128)} %param.8) | copy-start | bytes 40
  9.5 17.3 %all-to-all-start = ((f32[16,1,1536]{2,1,0:T(1,128)}), f32[16,1,1536]{2,1,0:T(1,128)S(1)}, u32[]{:S(2)}, u32[]{:S(2)}) async-start(f32[16,1,1536]{2,1,0:T(1,128)} %reshape.57), calls=%async_computation | async-start | bytes 196608 | tf_op jit(solution)/shard_map/all_to_all | solution.py:185
  20.8 3.4 %copy-start.1 = (s32[16]{0:T(128)S(1)}, s32[16]{0:T(128)}, u32[]{:S(2)}) copy-start(s32[16]{0:T(128)} %param.10) | copy-start | bytes 196
  48.0 172.2 %collective-permute-start = (f32[768,768]{1,0:T(8,128)}, f32[768,768]{1,0:T(8,128)S(1)}, u32[]{:S(2)}, u32[]{:S(2)}) collective-permute-start(f32[768,768]{1,0:T(8,128)} %get-tuple-element.47), channel_id=1, source_target_pairs={{1,0},{2,1},{3,2},{4,3},{5,4},{6,5},{7,6},{8,7},{9,8},{10,9},{11,1... | collective-permute-start | bytes 7077896 | tf_op jit(solution)/shard_map/ppermute | solution.py:14
  49.3 170.3 %collective-permute-start.1 = (f32[16,768]{1,0:T(8,128)S(1)}, f32[16,768]{1,0:T(8,128)S(1)}, u32[]{:S(2)}, u32[]{:S(2)}) collective-permute-start(f32[16,768]{1,0:T(8,128)S(1)} %broadcast_select_fusion.1), channel_id=1, source_target_pairs={{1,0},{2,1},{3,2},{4,3},{5,4},{6,5},{7,6},{8,7},{9,8},{10,9},{11,1... | collective-permute-start | bytes 147464 | tf_op jit(solution)/shard_map/ppermute | solution.py:14
where the time goes:
time: 226 us; the launch traced here: 225 us
  blocking collectives  168 us (74%)
  other arithmetic  20.9 us (9%)
  Pallas kernels  13.4 us (6%)
  starting transfers between devices  9.96 us (4%)
  local copies, waits for them, and re-layouts  7.97 us (4%)
  between operations  5.36 us (2%)
    psum x1, blocking collectives, local(): tip_total = lax.psum(tip_data + apex_schur_block, 'tm')  168 us
    pallas_call x1, Pallas kernels, assemble(): pl.pallas_call(assemble_kernel, grid=(total_reads // chunk,), in_specs=[p...  13.4 us
    broadcast_in_dim x3, other arithmetic, local(): return (sep_block[None], fill[None], sep_border[None], tip)  9.87 us
    all_to_all x1, starting transfers between devices, local(): lax.all_to_all(packed, 'tm', split_axis=2, concat_axis=1, tiled=True)  7.39 us
    unnamed x9, local copies, waits for them, and re-layouts  4.54 us
  transfers between devices with their start and end apart: 3, of which 0 were waited for; matrix products, arithmetic and copies ran while one was open for 3% of the time, Pallas kernels for 0%

commit v1 on v0

--- a/solution.py
+++ b/solution.py
@@ -12,6 +12,18 @@
     length = lax.axis_size(axis)
     pairs = [(i, i + by) for i in range(length) if 0 <= i + by < length]
     return lax.ppermute(x, axis, pairs)
+
+
+def butterfly_sum(x, axis):
+    length = lax.axis_size(axis)
+    if length & (length - 1):
+        return lax.psum(x, axis)
+    stride = 1
+    while stride < length:
+        pairs = [(i, i ^ stride) for i in range(length)]
+        x = x + lax.ppermute(x, axis, pairs)
+        stride *= 2
+    return x
 
 
 def matmul_high(left, right):
@@ -216,7 +228,7 @@
     from_right, from_right_side = passed_along((left_update, left_side), "tm", -1)
     sep_block = hessian[0] + prior_diag + schur_update + from_right
     sep_border = border[0] + lateral_block + from_right_side
-    tip_total = lax.psum(tip_data + apex_schur_block, "tm")
+    tip_total = butterfly_sum(tip_data + apex_schur_block, "tm")
     tip = tip_total + tau_fixed * jnp.eye(covars, dtype=jnp.float32)
     return (sep_block[None], fill[None], sep_border[None], tip)
 

time: 226 us -> 210 us (0.929)
  blocking collectives: 168 us -> 0 us
  Pallas kernels: 13.4 us -> 113 us
  starting transfers between devices: 9.96 us -> 38.3 us
  matrix products: 0 us -> 10.8 us
  waiting for transfers between devices: 0.01 us -> 8.23 us
  other arithmetic: 20.9 us -> 24.1 us
    psum x1 -> x0, blocking collectives: 168 us -> none  [local(): tip_total = lax.psum(tip_data + apex_schur_block, 'tm')]
    pallas_call x0 -> x1, Pallas kernels: none -> 100 us  [eliminate(): pl.pallas_call(eliminate_kernel, out_shape=[jax.ShapeDtypeStruct((mesh_wi...]
    ppermute x0 -> x4, starting transfers between devices: none -> 28.2 us  [butterfly_sum(): x = x + lax.ppermute(x, axis, pairs)]
    dot_general x0 -> x1, matrix products: none -> 10.8 us  [eliminate(): lax.dot_general(work[:, mesh_width:], solved, (((0,), (0,)), ((), ())), p...]
    ppermute x0 -> x4, waiting for transfers between devices: none -> 7.98 us  [butterfly_sum(): x = x + lax.ppermute(x, axis, pairs)]
    add x1 -> x5, other arithmetic: 0.01 us -> 2.68 us  [the longest x1 2.67 us: eliminate(): interior = hessian[1] + prior_diag]
    concatenate x0 -> x1, other arithmetic: none -> 2.6 us  [eliminate(): start = jnp.concatenate([interior, coupling_block, border[1].T], axis=1)]
    unnamed x9 -> x13, local copies, waits for them, and re-layouts: 4.54 us -> 4.55 us
  transfers between devices with their start and end apart: 3 -> 7, of which waited for: 0 -> 5; matrix products, arithmetic and copies ran while one was open for 3% -> 3% of each run, Pallas kernels for 0% -> 0%
where the time goes in v1:
time: 210 us; the launch traced here: 209 us
  Pallas kernels  113 us (54%)
  starting transfers between devices  38.3 us (18%)
  other arithmetic  24.1 us (11%)
  matrix products  10.8 us (5%)
  local copies, waits for them, and re-layouts  8.31 us (4%)
  waiting for transfers between devices  8.23 us (4%)
  between operations  5.35 us (3%)
    pallas_call x1, Pallas kernels, eliminate(): pl.pallas_call(eliminate_kernel, out_shape=[jax.ShapeDtypeStruct((mesh_wi...  100 us
    ppermute x4, starting transfers between devices, butterfly_sum(): x = x + lax.ppermute(x, axis, pairs)  28.2 us
    pallas_call x1, Pallas kernels, assemble(): pl.pallas_call(assemble_kernel, grid=(total_reads // chunk,), in_specs=[p...  13.4 us
    dot_general x1, matrix products, eliminate(): lax.dot_general(work[:, mesh_width:], solved, (((0,), (0,)), ((), ())), p...  10.8 us
    ppermute x4, waiting for transfers between devices, butterfly_sum(): x = x + lax.ppermute(x, axis, pairs)  7.98 us
    broadcast_in_dim x3, other arithmetic, local(): return (sep_block[None], fill[None], sep_border[None], tip)  7.83 us
    all_to_all x1, starting transfers between devices, local(): lax.all_to_all(packed, 'tm', split_axis=2, concat_axis=1, tiled=True)  7.39 us
    unnamed x13, local copies, waits for them, and re-layouts  4.55 us
  transfers between devices with their start and end apart: 7, of which 5 were waited for; matrix products, arithmetic and copies ran while one was open for 3% of the time, Pallas kernels for 0%

profile of v1, /device:TPU:0, one launch (start us, length us, event | category | flops | bytes accessed | tf_op | source)
XLA Modules:
  0.0 208.6 jit_solution(6828813780090422995)
XLA Ops:
  0.6 0.7 convert_element_type.16
  1.7 1.0 copy.30
  2.7 1.0 copy.31
  3.8 2.2 %fusion.12 = f32[1024,1,24]{2,1,0:T(1,128)S(1)} fusion(f32[16,1,1024]{0,1,2:T(1,128)S(1)} %copy.31, f32[4,1,1024]{0,1,2:T(1,128)S(1)} %copy.30, f32[4,1,1024]{0,1,2:T(1,128)S(1)} %copy.29), kind=kLoop, calls=%fused_computation.24 | loop fusion | flops 49152 | bytes 196608
  6.6 1.9 reduce
  8.5 1.0 reshape.57
  9.5 7.4 %all-to-all-start = ((f32[16,1,1536]{2,1,0:T(1,128)}), f32[16,1,1536]{2,1,0:T(1,128)S(1)}, u32[]{:S(2)}, u32[]{:S(2)}) async-start(f32[16,1,1536]{2,1,0:T(1,128)} %reshape.57), calls=%async_computation | async-start | bytes 196608 | tf_op jit(solution)/shard_map/all_to_all | solution.py:197
  16.9 0.6 fusion.10
  20.8 3.4 %broadcast_multiply_fusion = (f32[768,768]{1,0:T(8,128)S(1)}, f32[768,768]{1,0:T(8,128)}) fusion(f32[768,768]{1,0:T(8,128)} %param.9, f32[]{:T(128)} %bitcast.9, f32[]{:T(128)} %bitcast.7), kind=kLoop, calls=%fused_computation.12 | loop fusion | flops 1179648 | bytes 7077896 | tf_op jit(solution)/shard_map/mul | solution.py:205
  25.5 0.6 fusion.11
  26.8 0.9 reduce.1
  27.7 0.9 reshape.58
  28.9 13.4 %shard_map.93 = (f32[2,768,768]{2,1,0:T(8,128)}, f32[2,16,768]{2,1,0:T(8,128)S(1)}, f32[16,16]{1,0:T(8,128)S(1)}) custom-call(f32[1]{0:T(128)} %bitcast.4.end_ref, f32[24,1024]{1,0:T(8,128)S(1)} %bitcast.38), custom_call_target="tpu_custom_call" | custom-call | tf_op jit(solution)/shard_map/pallas_call | solution.py:86
  42.3 118.0 %conditional.1 = (f32[768,768]{1,0:T(8,128)}, f32[16,768]{1,0:T(8,128)S(1)}, f32[16,16]{1,0:T(8,128)S(1)}) conditional(s32[]{:T(128)} %convert_element_type.17, () %tuple.16, (f32[2,768,768]{2,1,0:T(8,128)}, f32[768,768]{1,0:T(8,128)}, f32[2,16,768]{2,1,0:T(8,128)S(1)}, f32[768,768]{1,0:T(8,128)S(1)}) %tuple.17), branch_computations={%region_1.2_spmd, %region_2.3_spmd} | conditional | flops 5668257792 | bytes 29690904 | solution.py:221
  42.6 2.7 %bitcast_add_fusion = f32[768,768]{1,0:T(8,128)S(1)} fusion(f32[768,768]{1,0:T(8,128)} %get-tuple-element.9, f32[2,768,768]{2,1,0:T(8,128)} %get-tuple-element.8), kind=kLoop, calls=%fused_computation.3 | loop fusion | flops 589824 | bytes 7077888 | tf_op jit(solution)/shard_map/cond/branch_1_fun/add | solution.py:170
  45.3 2.6 %pad_maximum_fusion.start_ref = f32[768,1552]{1,0:T(8,128)} fusion(f32[768,16]{1,0:T(8,128)S(1)} %slice_bitcast_fusion, f32[768,768]{1,0:T(8,128)S(1)} %get-tuple-element.10, f32[768,768]{1,0:T(8,128)S(1)} %bitcast_add_fusion), kind=kLoop, calls=%fused_computation | loop fusion | flops 2383872 | bytes 9535488 | tf_op jit(solution)/shard_map/cond/branch_1_fun/concatenate | solution.py:171
  47.9 100.0 %branch_1_fun.1 = (f32[768,1552]{1,0:T(8,128)}, f32[768,784]{1,0:T(8,128)}) custom-call(f32[768,1552]{1,0:T(8,128)} %pad_maximum_fusion.start_ref), custom_call_target="tpu_custom_call" | custom-call | tf_op jit(solution)/shard_map/cond/branch_1_fun/pallas_call | solution.py:173
  147.9 10.8 %fusion.2 = f32[784,784]{1,0:T(8,128)S(1)} fusion(f32[768,784]{1,0:T(8,128)} %get-tuple-element.13, f32[768,1552]{1,0:T(8,128)} %get-tuple-element.12), kind=kOutput, calls=%fused_computation.4 | convolution fusion | flops 5665284096 | bytes 7963648 | tf_op jit(solution)/shard_map/cond/branch_1_fun/dot_general | solution.py:184
  158.7 1.6 slice.39
  160.3 3.5 %select_bitcast_fusion = (f32[1,768,768]{2,1,0:T(8,128)}, f32[768,768]{1,0:T(8,128)S(1)}) fusion(f32[768,768]{1,0:T(8,128)} %get-tuple-element.26, f32[768,768]{1,0:T(8,128)S(1)} %get-tuple-element.48, pred[]{:T(512)} %bitcast.8, pred[]{:T(512)S(6)} %gt.3), kind=kLoop, calls=%fused_computation.10 | loop fusion | flops 1769472 | bytes 9437186 | tf_op jit(solution)/shard_map/broadcast_in_dim | solution.py:233
  163.8 1.4 collective-permute-start
  165.3 1.2 collective-permute-start.2
  166.5 3.9 %collective-permute-done.2 = f32[16,16]{1,0:T(8,128)S(1)} collective-permute-done((f32[16,16]{1,0:T(8,128)S(1)}, f32[16,16]{1,0:T(8,128)S(1)}, u32[]{:S(2)}, u32[]{:S(2)}) %collective-permute-start.2) | collective-permute-done | bytes 1056 | tf_op jit(solution)/shard_map/ppermute | solution.py:24
  170.4 1.6 collective-permute-start.3
  172.0 2.1 collective-permute-done.3
  174.1 22.5 %collective-permute-start.4 = (f32[16,16]{1,0:T(8,128)S(1)}, f32[16,16]{1,0:T(8,128)S(1)}, u32[]{:S(2)}, u32[]{:S(2)}) collective-permute-start(f32[16,16]{1,0:T(8,128)S(1)} %add.50), channel_id=1, source_target_pairs={{0,4},{1,5},{2,6},{3,7},{4,0},{5,1},{6,2},{7,3},{8,12},{9,13},{10,... | collective-permute-start | bytes 3080 | tf_op jit(solution)/shard_map/ppermute | solution.py:24
  196.6 1.6 collective-permute-done.4
  198.2 3.0 %collective-permute-start.5 = (f32[16,16]{1,0:T(8,128)S(1)}, f32[16,16]{1,0:T(8,128)S(1)}, u32[]{:S(2)}, u32[]{:S(2)}) collective-permute-start(f32[16,16]{1,0:T(8,128)S(1)} %add.51), channel_id=1, source_target_pairs={{0,8},{1,9},{2,10},{3,11},{4,12},{5,13},{6,14},{7,15},{8,0},{9,1},... | collective-permute-start | bytes 3080 | tf_op jit(solution)/shard_map/ppermute | solution.py:24
  201.2 1.3 collective-permute-start.1
  202.8 1.2 select_add_fusion
  204.3 0.6 fusion.9
  204.9 3.7 %fusion.7 = f32[1,768,768]{2,1,0:T(8,128)} fusion(f32[768,768]{1,0:T(8,128)S(1)} %collective-permute-done, f32[768,768]{1,0:T(8,128)} %get-tuple-element.26, f32[768,768]{1,0:T(8,128)S(1)} %copy-done, f32[2,768,768]{2,1,0:T(8,128)S(1)} %copy-done.1), kind=kLoop, calls=%fused_computation.9 | loop fusion | flops 1769472 | bytes 11796480 | tf_op jit(solution)/shard_map/broadcast_in_dim | solution.py:233
  (27 shorter events, 2.8 us)
Async XLA Ops:
  2.7 14.2 %copy-start.2 = (f32[3]{0:T(128)S(1)}, f32[3]{0:T(128)}, u32[]{:S(2)}) copy-start(f32[3]{0:T(128)} %param.8) | copy-start | bytes 40
  9.5 17.3 %all-to-all-start = ((f32[16,1,1536]{2,1,0:T(1,128)}), f32[16,1,1536]{2,1,0:T(1,128)S(1)}, u32[]{:S(2)}, u32[]{:S(2)}) async-start(f32[16,1,1536]{2,1,0:T(1,128)} %reshape.57), calls=%async_computation | async-start | bytes 196608 | tf_op jit(solution)/shard_map/all_to_all | solution.py:197
  20.8 3.4 %copy-start.3 = (s32[16]{0:T(128)S(1)}, s32[16]{0:T(128)}, u32[]{:S(2)}) copy-start(s32[16]{0:T(128)} %param.10) | copy-start | bytes 196
  160.3 44.6 %copy-start = (f32[768,768]{1,0:T(8,128)S(1)}, f32[768,768]{1,0:T(8,128)}, u32[]{:S(2)}) copy-start(f32[768,768]{1,0:T(8,128)} %get-tuple-element.49) | copy-start | bytes 7077892
  160.3 44.6 %copy-start.1 = (f32[2,768,768]{2,1,0:T(8,128)S(1)}, f32[2,768,768]{2,1,0:T(8,128)}, u32[]{:S(2)}) copy-start(f32[2,768,768]{2,1,0:T(8,128)} %get-tuple-element.24) | copy-start | bytes 14155780
  163.8 41.1 %collective-permute-start = (f32[768,768]{1,0:T(8,128)S(1)}, f32[768,768]{1,0:T(8,128)S(1)}, u32[]{:S(2)}, u32[]{:S(2)}) collective-permute-start(f32[768,768]{1,0:T(8,128)S(1)} %get-tuple-element.47), channel_id=1, source_target_pairs={{1,0},{2,1},{3,2},{4,3},{5,4},{6,5},{7,6},{8,7},{9,8},{10,9},{11,1... | collective-permute-start | bytes 7077896 | tf_op jit(solution)/shard_map/ppermute | solution.py:14
  165.3 5.1 %collective-permute-start.2 = (f32[16,16]{1,0:T(8,128)S(1)}, f32[16,16]{1,0:T(8,128)S(1)}, u32[]{:S(2)}, u32[]{:S(2)}) collective-permute-start(f32[16,16]{1,0:T(8,128)S(1)} %add.48), channel_id=1, source_target_pairs={{0,1},{1,0},{2,3},{3,2},{4,5},{5,4},{6,7},{7,6},{8,9},{9,8},{10,11... | collective-permute-start | bytes 3080 | tf_op jit(solution)/shard_map/ppermute | solution.py:24
  170.4 3.7 %collective-permute-start.3 = (f32[16,16]{1,0:T(8,128)S(1)}, f32[16,16]{1,0:T(8,128)S(1)}, u32[]{:S(2)}, u32[]{:S(2)}) collective-permute-start(f32[16,16]{1,0:T(8,128)S(1)} %add.49), channel_id=1, source_target_pairs={{0,2},{1,3},{2,0},{3,1},{4,6},{5,7},{6,4},{7,5},{8,10},{9,11},{10,... | collective-permute-start | bytes 3080 | tf_op jit(solution)/shard_map/ppermute | solution.py:24
  174.1 24.1 %collective-permute-start.4 = (f32[16,16]{1,0:T(8,128)S(1)}, f32[16,16]{1,0:T(8,128)S(1)}, u32[]{:S(2)}, u32[]{:S(2)}) collective-permute-start(f32[16,16]{1,0:T(8,128)S(1)} %add.50), channel_id=1, source_target_pairs={{0,4},{1,5},{2,6},{3,7},{4,0},{5,1},{6,2},{7,3},{8,12},{9,13},{10,... | collective-permute-start | bytes 3080 | tf_op jit(solution)/shard_map/ppermute | solution.py:24
  198.2 4.6 %collective-permute-start.5 = (f32[16,16]{1,0:T(8,128)S(1)}, f32[16,16]{1,0:T(8,128)S(1)}, u32[]{:S(2)}, u32[]{:S(2)}) collective-permute-start(f32[16,16]{1,0:T(8,128)S(1)} %add.51), channel_id=1, source_target_pairs={{0,8},{1,9},{2,10},{3,11},{4,12},{5,13},{6,14},{7,15},{8,0},{9,1},... | collective-permute-start | bytes 3080 | tf_op jit(solution)/shard_map/ppermute | solution.py:24
  201.2 3.1 %collective-permute-start.1 = (f32[16,768]{1,0:T(8,128)S(1)}, f32[16,768]{1,0:T(8,128)S(1)}, u32[]{:S(2)}, u32[]{:S(2)}) collective-permute-start(f32[16,768]{1,0:T(8,128)S(1)} %broadcast_select_fusion.1), channel_id=1, source_target_pairs={{1,0},{2,1},{3,2},{4,3},{5,4},{6,5},{7,6},{8,7},{9,8},{10,9},{11,1... | collective-permute-start | bytes 147464 | tf_op jit(solution)/shard_map/ppermute | solution.py:14

commit v2 on v1

--- a/solution.py
+++ b/solution.py
@@ -146,7 +146,7 @@
         block_ref[...] = update
         return carry
 
-    lax.fori_loop(0, size, body, 0)
+    lax.fori_loop(0, size, body, 0, unroll=4)
 
 
 def eliminate_kernel(start_ref, work_ref, solved_ref, block_ref):

time: 210 us -> 209 us (level)
  no operation moved by 1% of the time
where the time goes in v2:
time: 209 us; the launch traced here: 208 us
  Pallas kernels  113 us (54%)
  starting transfers between devices  38.3 us (18%)
  other arithmetic  24.1 us (12%)
  matrix products  10.8 us (5%)
  local copies, waits for them, and re-layouts  8.31 us (4%)
  waiting for transfers between devices  8.23 us (4%)
  between operations  5.35 us (3%)
    pallas_call x1, Pallas kernels, eliminate(): pl.pallas_call(eliminate_kernel, out_shape=[jax.ShapeDtypeStruct((mesh_wi...  99.7 us
    ppermute x4, starting transfers between devices, butterfly_sum(): x = x + lax.ppermute(x, axis, pairs)  28.2 us
    pallas_call x1, Pallas kernels, assemble(): pl.pallas_call(assemble_kernel, grid=(total_reads // chunk,), in_specs=[p...  13.4 us
    dot_general x1, matrix products, eliminate(): lax.dot_general(work[:, mesh_width:], solved, (((0,), (0,)), ((), ())), p...  10.8 us
    ppermute x4, waiting for transfers between devices, butterfly_sum(): x = x + lax.ppermute(x, axis, pairs)  7.98 us
    broadcast_in_dim x3, other arithmetic, local(): return (sep_block[None], fill[None], sep_border[None], tip)  7.83 us
    all_to_all x1, starting transfers between devices, local(): lax.all_to_all(packed, 'tm', split_axis=2, concat_axis=1, tiled=True)  7.39 us
    unnamed x13, local copies, waits for them, and re-layouts  4.55 us
  transfers between devices with their start and end apart: 7, of which 5 were waited for; matrix products, arithmetic and copies ran while one was open for 3% of the time, Pallas kernels for 0%

profile of v2, /device:TPU:0, one launch (start us, length us, event | category | flops | bytes accessed | tf_op | source)
XLA Modules:
  0.0 208.2 jit_solution(573563350635572399)
XLA Ops:
  0.6 0.7 convert_element_type.16
  1.7 1.0 copy.30
  2.7 1.0 copy.31
  3.8 2.2 %fusion.12 = f32[1024,1,24]{2,1,0:T(1,128)S(1)} fusion(f32[16,1,1024]{0,1,2:T(1,128)S(1)} %copy.31, f32[4,1,1024]{0,1,2:T(1,128)S(1)} %copy.30, f32[4,1,1024]{0,1,2:T(1,128)S(1)} %copy.29), kind=kLoop, calls=%fused_computation.24 | loop fusion | flops 49152 | bytes 196608
  6.6 1.9 reduce
  8.5 1.0 reshape.57
  9.5 7.4 %all-to-all-start = ((f32[16,1,1536]{2,1,0:T(1,128)}), f32[16,1,1536]{2,1,0:T(1,128)S(1)}, u32[]{:S(2)}, u32[]{:S(2)}) async-start(f32[16,1,1536]{2,1,0:T(1,128)} %reshape.57), calls=%async_computation | async-start | bytes 196608 | tf_op jit(solution)/shard_map/all_to_all | solution.py:197
  16.9 0.6 fusion.10
  20.8 3.4 %broadcast_multiply_fusion = (f32[768,768]{1,0:T(8,128)S(1)}, f32[768,768]{1,0:T(8,128)}) fusion(f32[768,768]{1,0:T(8,128)} %param.9, f32[]{:T(128)} %bitcast.9, f32[]{:T(128)} %bitcast.7), kind=kLoop, calls=%fused_computation.12 | loop fusion | flops 1179648 | bytes 7077896 | tf_op jit(solution)/shard_map/mul | solution.py:205
  25.5 0.6 fusion.11
  26.8 0.9 reduce.1
  27.7 0.9 reshape.58
  28.9 13.4 %shard_map.93 = (f32[2,768,768]{2,1,0:T(8,128)}, f32[2,16,768]{2,1,0:T(8,128)S(1)}, f32[16,16]{1,0:T(8,128)S(1)}) custom-call(f32[1]{0:T(128)} %bitcast.4.end_ref, f32[24,1024]{1,0:T(8,128)S(1)} %bitcast.38), custom_call_target="tpu_custom_call" | custom-call | tf_op jit(solution)/shard_map/pallas_call | solution.py:86
  42.3 117.6 %conditional.1 = (f32[768,768]{1,0:T(8,128)}, f32[16,768]{1,0:T(8,128)S(1)}, f32[16,16]{1,0:T(8,128)S(1)}) conditional(s32[]{:T(128)} %convert_element_type.17, () %tuple.16, (f32[2,768,768]{2,1,0:T(8,128)}, f32[768,768]{1,0:T(8,128)}, f32[2,16,768]{2,1,0:T(8,128)S(1)}, f32[768,768]{1,0:T(8,128)S(1)}) %tuple.17), branch_computations={%region_1.2_spmd, %region_2.3_spmd} | conditional | flops 5668257792 | bytes 29690904 | solution.py:221
  42.6 2.7 %bitcast_add_fusion = f32[768,768]{1,0:T(8,128)S(1)} fusion(f32[768,768]{1,0:T(8,128)} %get-tuple-element.9, f32[2,768,768]{2,1,0:T(8,128)} %get-tuple-element.8), kind=kLoop, calls=%fused_computation.3 | loop fusion | flops 589824 | bytes 7077888 | tf_op jit(solution)/shard_map/cond/branch_1_fun/add | solution.py:170
  45.3 2.6 %pad_maximum_fusion.start_ref = f32[768,1552]{1,0:T(8,128)} fusion(f32[768,16]{1,0:T(8,128)S(1)} %slice_bitcast_fusion, f32[768,768]{1,0:T(8,128)S(1)} %get-tuple-element.10, f32[768,768]{1,0:T(8,128)S(1)} %bitcast_add_fusion), kind=kLoop, calls=%fused_computation | loop fusion | flops 2383872 | bytes 9535488 | tf_op jit(solution)/shard_map/cond/branch_1_fun/concatenate | solution.py:171
  47.9 99.7 %branch_1_fun.1 = (f32[768,1552]{1,0:T(8,128)}, f32[768,784]{1,0:T(8,128)}) custom-call(f32[768,1552]{1,0:T(8,128)} %pad_maximum_fusion.start_ref), custom_call_target="tpu_custom_call" | custom-call | tf_op jit(solution)/shard_map/cond/branch_1_fun/pallas_call | solution.py:173
  147.5 10.8 %fusion.2 = f32[784,784]{1,0:T(8,128)S(1)} fusion(f32[768,784]{1,0:T(8,128)} %get-tuple-element.13, f32[768,1552]{1,0:T(8,128)} %get-tuple-element.12), kind=kOutput, calls=%fused_computation.4 | convolution fusion | flops 5665284096 | bytes 7963648 | tf_op jit(solution)/shard_map/cond/branch_1_fun/dot_general | solution.py:184
  158.3 1.6 slice.39
  159.9 3.5 %select_bitcast_fusion = (f32[1,768,768]{2,1,0:T(8,128)}, f32[768,768]{1,0:T(8,128)S(1)}) fusion(f32[768,768]{1,0:T(8,128)} %get-tuple-element.26, f32[768,768]{1,0:T(8,128)S(1)} %get-tuple-element.48, pred[]{:T(512)} %bitcast.8, pred[]{:T(512)S(6)} %gt.3), kind=kLoop, calls=%fused_computation.10 | loop fusion | flops 1769472 | bytes 9437186 | tf_op jit(solution)/shard_map/broadcast_in_dim | solution.py:233
  163.5 1.4 collective-permute-start
  164.9 1.2 collective-permute-start.2
  166.1 3.9 %collective-permute-done.2 = f32[16,16]{1,0:T(8,128)S(1)} collective-permute-done((f32[16,16]{1,0:T(8,128)S(1)}, f32[16,16]{1,0:T(8,128)S(1)}, u32[]{:S(2)}, u32[]{:S(2)}) %collective-permute-start.2) | collective-permute-done | bytes 1056 | tf_op jit(solution)/shard_map/ppermute | solution.py:24
  170.0 1.6 collective-permute-start.3
  171.6 2.1 collective-permute-done.3
  173.7 22.5 %collective-permute-start.4 = (f32[16,16]{1,0:T(8,128)S(1)}, f32[16,16]{1,0:T(8,128)S(1)}, u32[]{:S(2)}, u32[]{:S(2)}) collective-permute-start(f32[16,16]{1,0:T(8,128)S(1)} %add.50), channel_id=1, source_target_pairs={{0,4},{1,5},{2,6},{3,7},{4,0},{5,1},{6,2},{7,3},{8,12},{9,13},{10,... | collective-permute-start | bytes 3080 | tf_op jit(solution)/shard_map/ppermute | solution.py:24
  196.2 1.6 collective-permute-done.4
  197.8 3.0 %collective-permute-start.5 = (f32[16,16]{1,0:T(8,128)S(1)}, f32[16,16]{1,0:T(8,128)S(1)}, u32[]{:S(2)}, u32[]{:S(2)}) collective-permute-start(f32[16,16]{1,0:T(8,128)S(1)} %add.51), channel_id=1, source_target_pairs={{0,8},{1,9},{2,10},{3,11},{4,12},{5,13},{6,14},{7,15},{8,0},{9,1},... | collective-permute-start | bytes 3080 | tf_op jit(solution)/shard_map/ppermute | solution.py:24
  200.8 1.3 collective-permute-start.1
  202.4 1.2 select_add_fusion
  203.9 0.6 fusion.9
  204.5 3.7 %fusion.7 = f32[1,768,768]{2,1,0:T(8,128)} fusion(f32[768,768]{1,0:T(8,128)S(1)} %collective-permute-done, f32[768,768]{1,0:T(8,128)} %get-tuple-element.26, f32[768,768]{1,0:T(8,128)S(1)} %copy-done, f32[2,768,768]{2,1,0:T(8,128)S(1)} %copy-done.1), kind=kLoop, calls=%fused_computation.9 | loop fusion | flops 1769472 | bytes 11796480 | tf_op jit(solution)/shard_map/broadcast_in_dim | solution.py:233
  (27 shorter events, 2.8 us)
Async XLA Ops:
  2.7 14.2 %copy-start.2 = (f32[3]{0:T(128)S(1)}, f32[3]{0:T(128)}, u32[]{:S(2)}) copy-start(f32[3]{0:T(128)} %param.8) | copy-start | bytes 40
  9.5 17.3 %all-to-all-start = ((f32[16,1,1536]{2,1,0:T(1,128)}), f32[16,1,1536]{2,1,0:T(1,128)S(1)}, u32[]{:S(2)}, u32[]{:S(2)}) async-start(f32[16,1,1536]{2,1,0:T(1,128)} %reshape.57), calls=%async_computation | async-start | bytes 196608 | tf_op jit(solution)/shard_map/all_to_all | solution.py:197
  20.8 3.4 %copy-start.3 = (s32[16]{0:T(128)S(1)}, s32[16]{0:T(128)}, u32[]{:S(2)}) copy-start(s32[16]{0:T(128)} %param.10) | copy-start | bytes 196
  159.9 44.6 %copy-start = (f32[768,768]{1,0:T(8,128)S(1)}, f32[768,768]{1,0:T(8,128)}, u32[]{:S(2)}) copy-start(f32[768,768]{1,0:T(8,128)} %get-tuple-element.49) | copy-start | bytes 7077892
  159.9 44.6 %copy-start.1 = (f32[2,768,768]{2,1,0:T(8,128)S(1)}, f32[2,768,768]{2,1,0:T(8,128)}, u32[]{:S(2)}) copy-start(f32[2,768,768]{2,1,0:T(8,128)} %get-tuple-element.24) | copy-start | bytes 14155780
  163.5 41.1 %collective-permute-start = (f32[768,768]{1,0:T(8,128)S(1)}, f32[768,768]{1,0:T(8,128)S(1)}, u32[]{:S(2)}, u32[]{:S(2)}) collective-permute-start(f32[768,768]{1,0:T(8,128)S(1)} %get-tuple-element.47), channel_id=1, source_target_pairs={{1,0},{2,1},{3,2},{4,3},{5,4},{6,5},{7,6},{8,7},{9,8},{10,9},{11,1... | collective-permute-start | bytes 7077896 | tf_op jit(solution)/shard_map/ppermute | solution.py:14
  164.9 5.1 %collective-permute-start.2 = (f32[16,16]{1,0:T(8,128)S(1)}, f32[16,16]{1,0:T(8,128)S(1)}, u32[]{:S(2)}, u32[]{:S(2)}) collective-permute-start(f32[16,16]{1,0:T(8,128)S(1)} %add.48), channel_id=1, source_target_pairs={{0,1},{1,0},{2,3},{3,2},{4,5},{5,4},{6,7},{7,6},{8,9},{9,8},{10,11... | collective-permute-start | bytes 3080 | tf_op jit(solution)/shard_map/ppermute | solution.py:24
  170.0 3.7 %collective-permute-start.3 = (f32[16,16]{1,0:T(8,128)S(1)}, f32[16,16]{1,0:T(8,128)S(1)}, u32[]{:S(2)}, u32[]{:S(2)}) collective-permute-start(f32[16,16]{1,0:T(8,128)S(1)} %add.49), channel_id=1, source_target_pairs={{0,2},{1,3},{2,0},{3,1},{4,6},{5,7},{6,4},{7,5},{8,10},{9,11},{10,... | collective-permute-start | bytes 3080 | tf_op jit(solution)/shard_map/ppermute | solution.py:24
  173.7 24.1 %collective-permute-start.4 = (f32[16,16]{1,0:T(8,128)S(1)}, f32[16,16]{1,0:T(8,128)S(1)}, u32[]{:S(2)}, u32[]{:S(2)}) collective-permute-start(f32[16,16]{1,0:T(8,128)S(1)} %add.50), channel_id=1, source_target_pairs={{0,4},{1,5},{2,6},{3,7},{4,0},{5,1},{6,2},{7,3},{8,12},{9,13},{10,... | collective-permute-start | bytes 3080 | tf_op jit(solution)/shard_map/ppermute | solution.py:24
  197.8 4.6 %collective-permute-start.5 = (f32[16,16]{1,0:T(8,128)S(1)}, f32[16,16]{1,0:T(8,128)S(1)}, u32[]{:S(2)}, u32[]{:S(2)}) collective-permute-start(f32[16,16]{1,0:T(8,128)S(1)} %add.51), channel_id=1, source_target_pairs={{0,8},{1,9},{2,10},{3,11},{4,12},{5,13},{6,14},{7,15},{8,0},{9,1},... | collective-permute-start | bytes 3080 | tf_op jit(solution)/shard_map/ppermute | solution.py:24
  200.8 3.1 %collective-permute-start.1 = (f32[16,768]{1,0:T(8,128)S(1)}, f32[16,768]{1,0:T(8,128)S(1)}, u32[]{:S(2)}, u32[]{:S(2)}) collective-permute-start(f32[16,768]{1,0:T(8,128)S(1)} %broadcast_select_fusion.1), channel_id=1, source_target_pairs={{1,0},{2,1},{3,2},{4,3},{5,4},{6,5},{7,6},{8,7},{9,8},{10,9},{11,1... | collective-permute-start | bytes 147464 | tf_op jit(solution)/shard_map/ppermute | solution.py:14

commit v3 on v1

--- a/solution.py
+++ b/solution.py
@@ -24,6 +24,34 @@
         x = x + lax.ppermute(x, axis, pairs)
         stride *= 2
     return x
+
+
+def block_grid(mesh_width):
+    size = 128 if mesh_width % 128 == 0 else mesh_width
+    return size, mesh_width // size
+
+
+def lower_blocks(matrix):
+    size, count = block_grid(matrix.shape[0])
+    tiles = [
+        matrix[i * size : (i + 1) * size, j * size : (j + 1) * size]
+        for i in range(count)
+        for j in range(i + 1)
+    ]
+    return jnp.stack(tiles)
+
+
+def from_lower_blocks(packed, mesh_width):
+    size, count = block_grid(mesh_width)
+    index = {}
+    for i in range(count):
+        for j in range(i + 1):
+            index[i, j] = len(index)
+    rows = []
+    for i in range(count):
+        row = [packed[index[i, j]] if j <= i else packed[index[j, i]].T for j in range(count)]
+        rows.append(jnp.concatenate(row, axis=1))
+    return jnp.concatenate(rows, axis=0)
 
 
 def matmul_high(left, right):
@@ -225,7 +253,9 @@
     fill = jnp.where(has_left, jnp.where(local_length == 2, schur_update, coupling_block), 0.0)
     left_update = jnp.where(has_left, schur_update, 0.0)
     left_side = jnp.where(has_left, lateral_block, 0.0)
-    from_right, from_right_side = passed_along((left_update, left_side), "tm", -1)
+    packed_update = lower_blocks(left_update)
+    packed_update, from_right_side = passed_along((packed_update, left_side), "tm", -1)
+    from_right = from_lower_blocks(packed_update, mesh_width)
     sep_block = hessian[0] + prior_diag + schur_update + from_right
     sep_border = border[0] + lateral_block + from_right_side
     tip_total = butterfly_sum(tip_data + apex_schur_block, "tm")

time: 210 us -> 203 us (0.967)
  starting transfers between devices: 38.3 us -> 29.1 us
  local copies, waits for them, and re-layouts: 8.31 us -> 11.7 us
    ppermute x4, starting transfers between devices: 28.2 us -> 19.1 us  [butterfly_sum(): x = x + lax.ppermute(x, axis, pairs)]
    unnamed x13 -> x71, local copies, waits for them, and re-layouts: 4.55 us -> 7.05 us
  transfers between devices with their start and end apart: 7 -> 7, of which waited for: 5 -> 5; matrix products, arithmetic and copies ran while one was open for 3% -> 4% of each run, Pallas kernels for 0% -> 0%
where the time goes in v3:
time: 203 us; the launch traced here: 202 us
  Pallas kernels  113 us (56%)
  starting transfers between devices  29.1 us (14%)
  other arithmetic  24.5 us (12%)
  local copies, waits for them, and re-layouts  11.7 us (6%)
  matrix products  10.8 us (5%)
  waiting for transfers between devices  6.83 us (3%)
  between operations  5.83 us (3%)
    pallas_call x1, Pallas kernels, eliminate(): pl.pallas_call(eliminate_kernel, out_shape=[jax.ShapeDtypeStruct((mesh_wi...  100 us
    ppermute x4, starting transfers between devices, butterfly_sum(): x = x + lax.ppermute(x, axis, pairs)  19.1 us
    pallas_call x1, Pallas kernels, assemble(): pl.pallas_call(assemble_kernel, grid=(total_reads // chunk,), in_specs=[p...  13.4 us
    dot_general x1, matrix products, eliminate(): lax.dot_general(work[:, mesh_width:], solved, (((0,), (0,)), ((), ())), p...  10.8 us
    broadcast_in_dim x3, other arithmetic, local(): return (sep_block[None], fill[None], sep_border[None], tip)  8.38 us
    all_to_all x1, starting transfers between devices, local(): lax.all_to_all(packed, 'tm', split_axis=2, concat_axis=1, tiled=True)  7.39 us
    unnamed x71, local copies, waits for them, and re-layouts  7.05 us
    ppermute x4, waiting for transfers between devices, butterfly_sum(): x = x + lax.ppermute(x, axis, pairs)  6.57 us
  transfers between devices with their start and end apart: 7, of which 5 were waited for; matrix products, arithmetic and copies ran while one was open for 4% of the time, Pallas kernels for 0%

profile of v3, /device:TPU:0, one launch (start us, length us, event | category | flops | bytes accessed | tf_op | source)
XLA Modules:
  0.0 202.1 jit_solution(12914024096075301495)
XLA Ops:
  0.6 0.7 convert_element_type.16
  1.7 1.0 copy.84
  2.7 1.0 copy.85
  3.8 2.2 %fusion.16 = f32[1024,1,24]{2,1,0:T(1,128)S(1)} fusion(f32[16,1,1024]{0,1,2:T(1,128)S(1)} %copy.85, f32[4,1,1024]{0,1,2:T(1,128)S(1)} %copy.84, f32[4,1,1024]{0,1,2:T(1,128)S(1)} %copy.83), kind=kLoop, calls=%fused_computation.112 | loop fusion | flops 49152 | bytes 196608
  6.5 1.9 reduce
  8.4 1.0 reshape.57
  9.4 7.4 %all-to-all-start = ((f32[16,1,1536]{2,1,0:T(1,128)}), f32[16,1,1536]{2,1,0:T(1,128)S(1)}, u32[]{:S(2)}, u32[]{:S(2)}) async-start(f32[16,1,1536]{2,1,0:T(1,128)} %reshape.57), calls=%async_computation | async-start | bytes 196608 | tf_op jit(solution)/shard_map/all_to_all | solution.py:225
  16.8 0.6 fusion.14
  20.7 3.4 %broadcast_multiply_fusion = (f32[768,768]{1,0:T(8,128)S(1)}, f32[768,768]{1,0:T(8,128)}) fusion(f32[768,768]{1,0:T(8,128)} %param.9, f32[]{:T(128)} %bitcast.9, f32[]{:T(128)} %bitcast.7), kind=kLoop, calls=%fused_computation.12 | loop fusion | flops 1179648 | bytes 7077896 | tf_op jit(solution)/shard_map/mul | solution.py:233
  26.6 0.8 reduce.1
  27.4 0.9 reshape.58
  28.6 13.4 %shard_map.93 = (f32[2,768,768]{2,1,0:T(8,128)}, f32[2,16,768]{2,1,0:T(8,128)S(1)}, f32[16,16]{1,0:T(8,128)S(1)}) custom-call(f32[1]{0:T(128)} %bitcast.4.end_ref, f32[24,1024]{1,0:T(8,128)S(1)} %bitcast.218), custom_call_target="tpu_custom_call" | custom-call | tf_op jit(solution)/shard_map/pallas_call | solution.py:114
  42.0 118.0 %conditional.1 = (f32[768,768]{1,0:T(8,128)}, f32[16,768]{1,0:T(8,128)S(1)}, f32[16,16]{1,0:T(8,128)S(1)}) conditional(s32[]{:T(128)} %convert_element_type.17, () %tuple.16, (f32[2,768,768]{2,1,0:T(8,128)}, f32[768,768]{1,0:T(8,128)}, f32[2,16,768]{2,1,0:T(8,128)S(1)}, f32[768,768]{1,0:T(8,128)S(1)}) %tuple.17), branch_computations={%region_1.2_spmd, %region_2.3_spmd} | conditional | flops 5668257792 | bytes 29690904 | solution.py:249
  42.3 2.7 %bitcast_add_fusion = f32[768,768]{1,0:T(8,128)S(1)} fusion(f32[768,768]{1,0:T(8,128)} %get-tuple-element.9, f32[2,768,768]{2,1,0:T(8,128)} %get-tuple-element.8), kind=kLoop, calls=%fused_computation.3 | loop fusion | flops 589824 | bytes 7077888 | tf_op jit(solution)/shard_map/cond/branch_1_fun/add | solution.py:198
  45.0 2.6 %pad_maximum_fusion.start_ref = f32[768,1552]{1,0:T(8,128)} fusion(f32[768,16]{1,0:T(8,128)S(1)} %slice_bitcast_fusion, f32[768,768]{1,0:T(8,128)S(1)} %get-tuple-element.10, f32[768,768]{1,0:T(8,128)S(1)} %bitcast_add_fusion), kind=kLoop, calls=%fused_computation | loop fusion | flops 2383872 | bytes 9535488 | tf_op jit(solution)/shard_map/cond/branch_1_fun/concatenate | solution.py:199
  47.5 100.0 %branch_1_fun.1 = (f32[768,1552]{1,0:T(8,128)}, f32[768,784]{1,0:T(8,128)}) custom-call(f32[768,1552]{1,0:T(8,128)} %pad_maximum_fusion.start_ref), custom_call_target="tpu_custom_call" | custom-call | tf_op jit(solution)/shard_map/cond/branch_1_fun/pallas_call | solution.py:201
  147.6 10.8 %fusion.2 = f32[784,784]{1,0:T(8,128)S(1)} fusion(f32[768,784]{1,0:T(8,128)} %get-tuple-element.13, f32[768,1552]{1,0:T(8,128)} %get-tuple-element.12), kind=kOutput, calls=%fused_computation.4 | convolution fusion | flops 5665284096 | bytes 7963648 | tf_op jit(solution)/shard_map/cond/branch_1_fun/dot_general | solution.py:212
  158.4 1.6 slice.222
  160.0 3.4 %select_bitcast_fusion = (f32[1,768,768]{2,1,0:T(8,128)}, f32[768,768]{1,0:T(8,128)S(1)}) fusion(f32[768,768]{1,0:T(8,128)} %get-tuple-element.26, f32[768,768]{1,0:T(8,128)S(1)} %get-tuple-element.48, pred[]{:T(512)} %bitcast.8, pred[]{:T(512)S(6)} %gt.3), kind=kLoop, calls=%fused_computation.10 | loop fusion | flops 1769472 | bytes 9437186 | tf_op jit(solution)/shard_map/broadcast_in_dim | solution.py:263
  163.7 1.3 collective-permute-start
  165.0 1.2 collective-permute-start.2
  166.2 2.5 %collective-permute-done.2 = f32[16,16]{1,0:T(8,128)S(1)} collective-permute-done((f32[16,16]{1,0:T(8,128)S(1)}, f32[16,16]{1,0:T(8,128)S(1)}, u32[]{:S(2)}, u32[]{:S(2)}) %collective-permute-start.2) | collective-permute-done | bytes 1056 | tf_op jit(solution)/shard_map/ppermute | solution.py:24
  168.7 1.6 collective-permute-start.3
  170.3 2.1 %collective-permute-done.3 = f32[16,16]{1,0:T(8,128)S(1)} collective-permute-done((f32[16,16]{1,0:T(8,128)S(1)}, f32[16,16]{1,0:T(8,128)S(1)}, u32[]{:S(2)}, u32[]{:S(2)}) %collective-permute-start.3) | collective-permute-done | bytes 1056 | tf_op jit(solution)/shard_map/ppermute | solution.py:24
  172.4 13.1 %collective-permute-start.4 = (f32[16,16]{1,0:T(8,128)S(1)}, f32[16,16]{1,0:T(8,128)S(1)}, u32[]{:S(2)}, u32[]{:S(2)}) collective-permute-start(f32[16,16]{1,0:T(8,128)S(1)} %add.50), channel_id=1, source_target_pairs={{0,4},{1,5},{2,6},{3,7},{4,0},{5,1},{6,2},{7,3},{8,12},{9,13},{10,... | collective-permute-start | bytes 3080 | tf_op jit(solution)/shard_map/ppermute | solution.py:24
  185.5 1.6 collective-permute-done.4
  187.1 3.2 %collective-permute-start.5 = (f32[16,16]{1,0:T(8,128)S(1)}, f32[16,16]{1,0:T(8,128)S(1)}, u32[]{:S(2)}, u32[]{:S(2)}) collective-permute-start(f32[16,16]{1,0:T(8,128)S(1)} %add.51), channel_id=1, source_target_pairs={{0,8},{1,9},{2,10},{3,11},{4,12},{5,13},{6,14},{7,15},{8,0},{9,1},... | collective-permute-start | bytes 3080 | tf_op jit(solution)/shard_map/ppermute | solution.py:24
  190.4 1.3 collective-permute-start.1
  192.0 1.2 select_add_fusion
  193.5 0.6 fusion.12
  196.5 1.3 copy-done
  197.8 4.4 %fusion.7 = f32[1,768,768]{2,1,0:T(8,128)} fusion(f32[768,768]{1,0:T(8,128)S(1)} %fusion.8, f32[768,768]{1,0:T(8,128)} %get-tuple-element.26, f32[768,768]{1,0:T(8,128)S(1)} %copy-done, f32[2,768,768]{2,1,0:T(8,128)} %get-tuple-element.24), kind=kLoop, calls=%fused_computation.9 | loop fusion | flops 1769472 | bytes 11796480 | tf_op jit(solution)/shard_map/broadcast_in_dim | solution.py:263
  (97 shorter events, 5.4 us)
Async XLA Ops:
  2.7 14.1 %copy-start.1 = (f32[3]{0:T(128)S(1)}, f32[3]{0:T(128)}, u32[]{:S(2)}) copy-start(f32[3]{0:T(128)} %param.8) | copy-start | bytes 40
  9.4 17.2 %all-to-all-start = ((f32[16,1,1536]{2,1,0:T(1,128)}), f32[16,1,1536]{2,1,0:T(1,128)S(1)}, u32[]{:S(2)}, u32[]{:S(2)}) async-start(f32[16,1,1536]{2,1,0:T(1,128)} %reshape.57), calls=%async_computation | async-start | bytes 196608 | tf_op jit(solution)/shard_map/all_to_all | solution.py:225
  20.7 3.4 %copy-start.2 = (s32[16]{0:T(128)S(1)}, s32[16]{0:T(128)}, u32[]{:S(2)}) copy-start(s32[16]{0:T(128)} %param.10) | copy-start | bytes 196
  163.7 30.4 %collective-permute-start = (f32[21,128,128]{2,1,0:T(8,128)S(1)}, f32[21,128,128]{2,1,0:T(8,128)S(1)}, u32[]{:S(2)}, u32[]{:S(2)}) collective-permute-start(f32[21,128,128]{2,1,0:T(8,128)S(1)} %constant_dynamic-update-slice_fusion), channel_id=1, source_target_pairs={{1,0},{2,1},{3,2},{4,3},{5,4},{6,5},{7,6},{8,7},{9,8},{10,9},{11,1... | collective-permute-start | bytes 4128776 | tf_op jit(solution)/shard_map/ppermute | solution.py:14
  165.0 3.7 %collective-permute-start.2 = (f32[16,16]{1,0:T(8,128)S(1)}, f32[16,16]{1,0:T(8,128)S(1)}, u32[]{:S(2)}, u32[]{:S(2)}) collective-permute-start(f32[16,16]{1,0:T(8,128)S(1)} %add.48), channel_id=1, source_target_pairs={{0,1},{1,0},{2,3},{3,2},{4,5},{5,4},{6,7},{7,6},{8,9},{9,8},{10,11... | collective-permute-start | bytes 3080 | tf_op jit(solution)/shard_map/ppermute | solution.py:24
  168.7 3.7 %collective-permute-start.3 = (f32[16,16]{1,0:T(8,128)S(1)}, f32[16,16]{1,0:T(8,128)S(1)}, u32[]{:S(2)}, u32[]{:S(2)}) collective-permute-start(f32[16,16]{1,0:T(8,128)S(1)} %add.49), channel_id=1, source_target_pairs={{0,2},{1,3},{2,0},{3,1},{4,6},{5,7},{6,4},{7,5},{8,10},{9,11},{10,... | collective-permute-start | bytes 3080 | tf_op jit(solution)/shard_map/ppermute | solution.py:24
  172.4 14.7 %collective-permute-start.4 = (f32[16,16]{1,0:T(8,128)S(1)}, f32[16,16]{1,0:T(8,128)S(1)}, u32[]{:S(2)}, u32[]{:S(2)}) collective-permute-start(f32[16,16]{1,0:T(8,128)S(1)} %add.50), channel_id=1, source_target_pairs={{0,4},{1,5},{2,6},{3,7},{4,0},{5,1},{6,2},{7,3},{8,12},{9,13},{10,... | collective-permute-start | bytes 3080 | tf_op jit(solution)/shard_map/ppermute | solution.py:24
  187.1 4.9 %collective-permute-start.5 = (f32[16,16]{1,0:T(8,128)S(1)}, f32[16,16]{1,0:T(8,128)S(1)}, u32[]{:S(2)}, u32[]{:S(2)}) collective-permute-start(f32[16,16]{1,0:T(8,128)S(1)} %add.51), channel_id=1, source_target_pairs={{0,8},{1,9},{2,10},{3,11},{4,12},{5,13},{6,14},{7,15},{8,0},{9,1},... | collective-permute-start | bytes 3080 | tf_op jit(solution)/shard_map/ppermute | solution.py:24
  190.4 3.1 %collective-permute-start.1 = (f32[16,768]{1,0:T(8,128)S(1)}, f32[16,768]{1,0:T(8,128)S(1)}, u32[]{:S(2)}, u32[]{:S(2)}) collective-permute-start(f32[16,768]{1,0:T(8,128)S(1)} %broadcast_select_fusion.1), channel_id=1, source_target_pairs={{1,0},{2,1},{3,2},{4,3},{5,4},{6,5},{7,6},{8,7},{9,8},{10,9},{11,1... | collective-permute-start | bytes 147464 | tf_op jit(solution)/shard_map/ppermute | solution.py:14
  196.1 1.7 copy-start

commit v4 on v3

--- a/solution.py
+++ b/solution.py
@@ -163,7 +163,7 @@
     def body(k, carry):
         current = block_ref[...]
         row = block_ref[pl.ds(k, 1), :]
-        col = jnp.sum(jnp.where(lane == k, current, 0.0), axis=1, keepdims=True)
+        col = jnp.transpose(jnp.broadcast_to(row, (8, size)))[:, 0:1]
         pivot = jnp.sum(jnp.where(lane_row == k, row, 0.0), axis=1, keepdims=True)
         inverse = 1.0 / pivot
         scaled_row = row * inverse

time: 203 us -> 316 us (1.56)
  Pallas kernels: 113 us -> 226 us
  starting transfers between devices: 29.1 us -> 15 us
  waiting for transfers between devices: 6.83 us -> 20.9 us
    pallas_call x1, Pallas kernels: 100 us -> 212 us  [eliminate(): pl.pallas_call(eliminate_kernel, out_shape=[jax.ShapeDtypeStruct((mesh_wi...]
    ppermute x4, waiting for transfers between devices: 6.57 us -> 20.9 us  [butterfly_sum(): x = x + lax.ppermute(x, axis, pairs)]
    ppermute x4, starting transfers between devices: 19.1 us -> 5.07 us  [butterfly_sum(): x = x + lax.ppermute(x, axis, pairs)]
  transfers between devices with their start and end apart: 7 -> 7, of which waited for: 5 -> 4; matrix products, arithmetic and copies ran while one was open for 4% -> 2% of each run, Pallas kernels for 0% -> 0%
where the time goes in v4:
time: 316 us; the launch traced here: 314 us
  Pallas kernels  226 us (72%)
  other arithmetic  24.5 us (8%)
  waiting for transfers between devices  20.9 us (7%)
  starting transfers between devices  15 us (5%)
  local copies, waits for them, and re-layouts  11.7 us (4%)
  matrix products  10.8 us (3%)
  between operations  5.83 us (2%)
    pallas_call x1, Pallas kernels, eliminate(): pl.pallas_call(eliminate_kernel, out_shape=[jax.ShapeDtypeStruct((mesh_wi...  212 us
    ppermute x4, waiting for transfers between devices, butterfly_sum(): x = x + lax.ppermute(x, axis, pairs)  20.9 us
    pallas_call x1, Pallas kernels, assemble(): pl.pallas_call(assemble_kernel, grid=(total_reads // chunk,), in_specs=[p...  13.4 us
    dot_general x1, matrix products, eliminate(): lax.dot_general(work[:, mesh_width:], solved, (((0,), (0,)), ((), ())), p...  10.8 us
    broadcast_in_dim x3, other arithmetic, local(): return (sep_block[None], fill[None], sep_border[None], tip)  8.38 us
    all_to_all x1, starting transfers between devices, local(): lax.all_to_all(packed, 'tm', split_axis=2, concat_axis=1, tiled=True)  7.39 us
    unnamed x71, local copies, waits for them, and re-layouts  7.05 us
  transfers between devices with their start and end apart: 7, of which 4 were waited for; matrix products, arithmetic and copies ran while one was open for 2% of the time, Pallas kernels for 0%

profile of v4, /device:TPU:0, one launch (start us, length us, event | category | flops | bytes accessed | tf_op | source)
XLA Modules:
  0.0 314.3 jit_solution(478048391468331426)
XLA Ops:
  0.6 0.7 convert_element_type.16
  1.7 1.0 copy.84
  2.7 1.0 copy.85
  3.8 2.2 fusion.16
  6.5 1.9 reduce
  8.4 1.0 reshape.57
  9.4 7.4 %all-to-all-start = ((f32[16,1,1536]{2,1,0:T(1,128)}), f32[16,1,1536]{2,1,0:T(1,128)S(1)}, u32[]{:S(2)}, u32[]{:S(2)}) async-start(f32[16,1,1536]{2,1,0:T(1,128)} %reshape.57), calls=%async_computation | async-start | bytes 196608 | tf_op jit(solution)/shard_map/all_to_all | solution.py:225
  16.8 0.6 fusion.14
  20.7 3.4 %broadcast_multiply_fusion = (f32[768,768]{1,0:T(8,128)S(1)}, f32[768,768]{1,0:T(8,128)}) fusion(f32[768,768]{1,0:T(8,128)} %param.9, f32[]{:T(128)} %bitcast.9, f32[]{:T(128)} %bitcast.7), kind=kLoop, calls=%fused_computation.12 | loop fusion | flops 1179648 | bytes 7077896 | tf_op jit(solution)/shard_map/mul | solution.py:233
  26.6 0.8 reduce.1
  27.4 0.9 reshape.58
  28.6 13.4 %shard_map.93 = (f32[2,768,768]{2,1,0:T(8,128)}, f32[2,16,768]{2,1,0:T(8,128)S(1)}, f32[16,16]{1,0:T(8,128)S(1)}) custom-call(f32[1]{0:T(128)} %bitcast.4.end_ref, f32[24,1024]{1,0:T(8,128)S(1)} %bitcast.218), custom_call_target="tpu_custom_call" | custom-call | tf_op jit(solution)/shard_map/pallas_call | solution.py:114
  42.0 230.2 %conditional.1 = (f32[768,768]{1,0:T(8,128)}, f32[16,768]{1,0:T(8,128)S(1)}, f32[16,16]{1,0:T(8,128)S(1)}) conditional(s32[]{:T(128)} %convert_element_type.17, () %tuple.16, (f32[2,768,768]{2,1,0:T(8,128)}, f32[768,768]{1,0:T(8,128)}, f32[2,16,768]{2,1,0:T(8,128)S(1)}, f32[768,768]{1,0:T(8,128)S(1)}) %tuple.17), branch_computations={%region_1.2_spmd, %region_2.3_spmd} | conditional | flops 5668257792 | bytes 29690904 | solution.py:249
  42.3 2.7 bitcast_add_fusion
  45.0 2.6 pad_maximum_fusion.start_ref
  47.5 212.2 %branch_1_fun.1 = (f32[768,1552]{1,0:T(8,128)}, f32[768,784]{1,0:T(8,128)}) custom-call(f32[768,1552]{1,0:T(8,128)} %pad_maximum_fusion.start_ref), custom_call_target="tpu_custom_call" | custom-call | tf_op jit(solution)/shard_map/cond/branch_1_fun/pallas_call | solution.py:201
  259.7 10.8 %fusion.2 = f32[784,784]{1,0:T(8,128)S(1)} fusion(f32[768,784]{1,0:T(8,128)} %get-tuple-element.13, f32[768,1552]{1,0:T(8,128)} %get-tuple-element.12), kind=kOutput, calls=%fused_computation.4 | convolution fusion | flops 5665284096 | bytes 7963648 | tf_op jit(solution)/shard_map/cond/branch_1_fun/dot_general | solution.py:212
  270.6 1.6 slice.222
  272.2 3.4 %select_bitcast_fusion = (f32[1,768,768]{2,1,0:T(8,128)}, f32[768,768]{1,0:T(8,128)S(1)}) fusion(f32[768,768]{1,0:T(8,128)} %get-tuple-element.26, f32[768,768]{1,0:T(8,128)S(1)} %get-tuple-element.48, pred[]{:T(512)} %bitcast.8, pred[]{:T(512)S(6)} %gt.3), kind=kLoop, calls=%fused_computation.10 | loop fusion | flops 1769472 | bytes 9437186 | tf_op jit(solution)/shard_map/broadcast_in_dim | solution.py:263
  275.8 1.3 collective-permute-start
  277.1 1.2 collective-permute-start.2
  278.3 2.5 collective-permute-done.2
  281.0 15.2 %collective-permute-done.3 = f32[16,16]{1,0:T(8,128)S(1)} collective-permute-done((f32[16,16]{1,0:T(8,128)S(1)}, f32[16,16]{1,0:T(8,128)S(1)}, u32[]{:S(2)}, u32[]{:S(2)}) %collective-permute-start.3) | collective-permute-done | bytes 1056 | tf_op jit(solution)/shard_map/ppermute | solution.py:24
  296.2 1.4 collective-permute-start.4
  297.6 2.2 collective-permute-done.4
  299.9 2.3 collective-permute-start.5
  302.2 1.3 collective-permute-start.1
  303.5 1.0 collective-permute-done.5
  304.4 1.2 select_add_fusion
  305.7 0.6 fusion.12
  308.7 1.3 copy-done
  310.0 4.4 %fusion.7 = f32[1,768,768]{2,1,0:T(8,128)} fusion(f32[768,768]{1,0:T(8,128)S(1)} %fusion.8, f32[768,768]{1,0:T(8,128)} %get-tuple-element.26, f32[768,768]{1,0:T(8,128)S(1)} %copy-done, f32[2,768,768]{2,1,0:T(8,128)} %get-tuple-element.24), kind=kLoop, calls=%fused_computation.9 | loop fusion | flops 1769472 | bytes 11796480 | tf_op jit(solution)/shard_map/broadcast_in_dim | solution.py:263
  (97 shorter events, 5.0 us)
Async XLA Ops:
  2.7 14.1 %copy-start.1 = (f32[3]{0:T(128)S(1)}, f32[3]{0:T(128)}, u32[]{:S(2)}) copy-start(f32[3]{0:T(128)} %param.8) | copy-start | bytes 40
  9.4 17.2 %all-to-all-start = ((f32[16,1,1536]{2,1,0:T(1,128)}), f32[16,1,1536]{2,1,0:T(1,128)S(1)}, u32[]{:S(2)}, u32[]{:S(2)}) async-start(f32[16,1,1536]{2,1,0:T(1,128)} %reshape.57), calls=%async_computation | async-start | bytes 196608 | tf_op jit(solution)/shard_map/all_to_all | solution.py:225
  20.7 3.4 %copy-start.2 = (s32[16]{0:T(128)S(1)}, s32[16]{0:T(128)}, u32[]{:S(2)}) copy-start(s32[16]{0:T(128)} %param.10) | copy-start | bytes 196
  275.8 30.5 %collective-permute-start = (f32[21,128,128]{2,1,0:T(8,128)S(1)}, f32[21,128,128]{2,1,0:T(8,128)S(1)}, u32[]{:S(2)}, u32[]{:S(2)}) collective-permute-start(f32[21,128,128]{2,1,0:T(8,128)S(1)} %constant_dynamic-update-slice_fusion), channel_id=1, source_target_pairs={{1,0},{2,1},{3,2},{4,3},{5,4},{6,5},{7,6},{8,7},{9,8},{10,9},{11,1... | collective-permute-start | bytes 4128776 | tf_op jit(solution)/shard_map/ppermute | solution.py:14
  277.1 3.7 %collective-permute-start.2 = (f32[16,16]{1,0:T(8,128)S(1)}, f32[16,16]{1,0:T(8,128)S(1)}, u32[]{:S(2)}, u32[]{:S(2)}) collective-permute-start(f32[16,16]{1,0:T(8,128)S(1)} %add.48), channel_id=1, source_target_pairs={{0,1},{1,0},{2,3},{3,2},{4,5},{5,4},{6,7},{7,6},{8,9},{9,8},{10,11... | collective-permute-start | bytes 3080 | tf_op jit(solution)/shard_map/ppermute | solution.py:24
  280.9 15.3 %collective-permute-start.3 = (f32[16,16]{1,0:T(8,128)S(1)}, f32[16,16]{1,0:T(8,128)S(1)}, u32[]{:S(2)}, u32[]{:S(2)}) collective-permute-start(f32[16,16]{1,0:T(8,128)S(1)} %add.49), channel_id=1, source_target_pairs={{0,2},{1,3},{2,0},{3,1},{4,6},{5,7},{6,4},{7,5},{8,10},{9,11},{10,... | collective-permute-start | bytes 3080 | tf_op jit(solution)/shard_map/ppermute | solution.py:24
  296.2 3.7 %collective-permute-start.4 = (f32[16,16]{1,0:T(8,128)S(1)}, f32[16,16]{1,0:T(8,128)S(1)}, u32[]{:S(2)}, u32[]{:S(2)}) collective-permute-start(f32[16,16]{1,0:T(8,128)S(1)} %add.50), channel_id=1, source_target_pairs={{0,4},{1,5},{2,6},{3,7},{4,0},{5,1},{6,2},{7,3},{8,12},{9,13},{10,... | collective-permute-start | bytes 3080 | tf_op jit(solution)/shard_map/ppermute | solution.py:24
  299.9 4.5 %collective-permute-start.5 = (f32[16,16]{1,0:T(8,128)S(1)}, f32[16,16]{1,0:T(8,128)S(1)}, u32[]{:S(2)}, u32[]{:S(2)}) collective-permute-start(f32[16,16]{1,0:T(8,128)S(1)} %add.51), channel_id=1, source_target_pairs={{0,8},{1,9},{2,10},{3,11},{4,12},{5,13},{6,14},{7,15},{8,0},{9,1},... | collective-permute-start | bytes 3080 | tf_op jit(solution)/shard_map/ppermute | solution.py:24
  302.2 3.5 %collective-permute-start.1 = (f32[16,768]{1,0:T(8,128)S(1)}, f32[16,768]{1,0:T(8,128)S(1)}, u32[]{:S(2)}, u32[]{:S(2)}) collective-permute-start(f32[16,768]{1,0:T(8,128)S(1)} %broadcast_select_fusion.1), channel_id=1, source_target_pairs={{1,0},{2,1},{3,2},{4,3},{5,4},{6,5},{7,6},{8,7},{9,8},{10,9},{11,1... | collective-permute-start | bytes 147464 | tf_op jit(solution)/shard_map/ppermute | solution.py:14
  308.3 1.7 copy-start

commit v5 on v3

--- a/solution.py
+++ b/solution.py
@@ -141,6 +141,12 @@
     return high, low
 
 
+def kept_split(value):
+    high = lax.reduce_precision(value, exponent_bits=8, mantissa_bits=7)
+    low = value - high
+    return high.astype(jnp.bfloat16), low.astype(jnp.bfloat16)
+
+
 def split_matmul(left, right):
     left_hi, left_lo = split_parts(left)
     right_hi, right_lo = split_parts(right)
@@ -209,8 +215,12 @@
         scratch_shapes=[pltpu.VMEM((block_size, block_size), jnp.float32)],
         compiler_params=pltpu.CompilerParams(vmem_limit_bytes=60 * 1024 * 1024),
     )(start)
-    schur = -lax.dot_general(
-        work[:, mesh_width:], solved, (((0,), (0,)), ((), ())), precision=HIGHEST
+    rhs_hi, rhs_lo = kept_split(work[:, mesh_width:])
+    solved_hi, solved_lo = kept_split(solved)
+    schur = -(
+        contract_rows(rhs_hi, solved_hi)
+        + contract_rows(rhs_hi, solved_lo)
+        + contract_rows(rhs_lo, solved_hi)
     )
     schur_update = schur[:mesh_width, :mesh_width]
     lateral_block = schur[mesh_width:, :mesh_width]

time: 203 us -> 201 us (level)
  starting transfers between devices: 29.1 us -> 129 us
  Pallas kernels: 113 us -> 13.4 us
  waiting for transfers between devices: 6.83 us -> 20.6 us
  matrix products: 10.8 us -> 0 us
  other arithmetic: 24.5 us -> 19.4 us
    pallas_call x1 -> x0, Pallas kernels: 100 us -> none  [eliminate(): pl.pallas_call(eliminate_kernel, out_shape=[jax.ShapeDtypeStruct((mesh_wi...]
    ppermute x4, starting transfers between devices: 19.1 us -> 119 us  [butterfly_sum(): x = x + lax.ppermute(x, axis, pairs)]
    ppermute x4, waiting for transfers between devices: 6.57 us -> 20.6 us  [butterfly_sum(): x = x + lax.ppermute(x, axis, pairs)]
    dot_general x1 -> x0, matrix products: 10.8 us -> none  [eliminate(): lax.dot_general(work[:, mesh_width:], solved, (((0,), (0,)), ((), ())), p...]
    add x1 -> x0, other arithmetic: 2.67 us -> none  [eliminate(): interior = hessian[1] + prior_diag]
    concatenate x1 -> x0, other arithmetic: 2.6 us -> none  [eliminate(): start = jnp.concatenate([interior, coupling_block, border[1].T], axis=1)]
  transfers between devices with their start and end apart: 7 -> 7, of which waited for: 5 -> 4; matrix products, arithmetic and copies ran while one was open for 4% -> 4% of each run, Pallas kernels for 0% -> 0%
where the time goes in v5:
time: 201 us; the launch traced here: 200 us
  starting transfers between devices  129 us (64%)
  waiting for transfers between devices  20.6 us (10%)
  other arithmetic  19.4 us (10%)
  Pallas kernels  13.4 us (7%)
  local copies, waits for them, and re-layouts  11.4 us (6%)
  between operations  5.9 us (3%)
    ppermute x4, starting transfers between devices, butterfly_sum(): x = x + lax.ppermute(x, axis, pairs)  119 us
    ppermute x4, waiting for transfers between devices, butterfly_sum(): x = x + lax.ppermute(x, axis, pairs)  20.6 us
    pallas_call x1, Pallas kernels, assemble(): pl.pallas_call(assemble_kernel, grid=(total_reads // chunk,), in_specs=[p...  13.4 us
    broadcast_in_dim x3, other arithmetic, local(): return (sep_block[None], fill[None], sep_border[None], tip)  8.38 us
    all_to_all x1, starting transfers between devices, local(): lax.all_to_all(packed, 'tm', split_axis=2, concat_axis=1, tiled=True)  7.39 us
    unnamed x71, local copies, waits for them, and re-layouts  7.11 us
    unnamed x2, other arithmetic  4.14 us
  transfers between devices with their start and end apart: 7, of which 4 were waited for; matrix products, arithmetic and copies ran while one was open for 4% of the time, Pallas kernels for 0%

profile of v5, /device:TPU:0, one launch (start us, length us, event | category | flops | bytes accessed | tf_op | source)
XLA Modules:
  0.0 199.7 jit_solution(757085671198304955)
XLA Ops:
  0.6 0.7 convert_element_type.28
  1.4 0.3 copy.83
  1.7 1.0 copy.84
  2.7 1.0 copy.85
  3.8 2.2 %fusion.17 = f32[1024,1,24]{2,1,0:T(1,128)S(1)} fusion(f32[16,1,1024]{0,1,2:T(1,128)S(1)} %copy.85, f32[4,1,1024]{0,1,2:T(1,128)S(1)} %copy.84, f32[4,1,1024]{0,1,2:T(1,128)S(1)} %copy.83), kind=kLoop, calls=%fused_computation.118 | loop fusion | flops 49152 | bytes 196608
  6.0 0.6 broadcast.22
  6.6 1.9 reduce
  8.5 1.0 reshape.57
  9.6 7.4 %all-to-all-start = ((f32[16,1,1536]{2,1,0:T(1,128)}), f32[16,1,1536]{2,1,0:T(1,128)S(1)}, u32[]{:S(2)}, u32[]{:S(2)}) async-start(f32[16,1,1536]{2,1,0:T(1,128)} %reshape.57), calls=%async_computation | async-start | bytes 196608 | tf_op jit(solution)/shard_map/all_to_all | solution.py:235
  17.0 0.6 fusion.15
  20.8 3.4 %broadcast_multiply_fusion = (f32[768,768]{1,0:T(8,128)S(1)}, f32[768,768]{1,0:T(8,128)}) fusion(f32[768,768]{1,0:T(8,128)} %param.9, f32[]{:T(128)} %bitcast.9, f32[]{:T(128)} %bitcast.7), kind=kLoop, calls=%fused_computation.18 | loop fusion | flops 1179648 | bytes 7077896 | tf_op jit(solution)/shard_map/mul | solution.py:243
  24.2 0.6 dynamic_slice.7
  25.6 0.6 fusion.16
  26.8 0.9 reduce.1
  27.7 0.9 reshape.58
  28.9 13.4 %shard_map.93 = (f32[2,768,768]{2,1,0:T(8,128)}, f32[2,16,768]{2,1,0:T(8,128)S(1)}, f32[16,16]{1,0:T(8,128)S(1)}) custom-call(f32[1]{0:T(128)} %bitcast.4.end_ref, f32[24,1024]{1,0:T(8,128)S(1)} %bitcast.217), custom_call_target="tpu_custom_call" | custom-call | tf_op jit(solution)/shard_map/pallas_call | solution.py:114
  42.2 1.6 conditional.1
  42.3 1.6 broadcast.13
  43.8 3.4 %select_bitcast_fusion = (f32[1,768,768]{2,1,0:T(8,128)}, f32[768,768]{1,0:T(8,128)S(1)}) fusion(f32[768,768]{1,0:T(8,128)} %get-tuple-element.26, f32[768,768]{1,0:T(8,128)S(1)} %get-tuple-element.48, pred[]{:T(512)} %bitcast.8, pred[]{:T(512)S(6)} %gt.3), kind=kLoop, calls=%fused_computation.16 | loop fusion | flops 1769472 | bytes 9437186 | tf_op jit(solution)/shard_map/broadcast_in_dim | solution.py:273
  47.5 1.3 collective-permute-start
  48.8 114.8 %collective-permute-start.2 = (f32[16,16]{1,0:T(8,128)S(1)}, f32[16,16]{1,0:T(8,128)S(1)}, u32[]{:S(2)}, u32[]{:S(2)}) collective-permute-start(f32[16,16]{1,0:T(8,128)S(1)} %add.54), channel_id=1, source_target_pairs={{0,1},{1,0},{2,3},{3,2},{4,5},{5,4},{6,7},{7,6},{8,9},{9,8},{10,11... | collective-permute-start | bytes 3080 | tf_op jit(solution)/shard_map/ppermute | solution.py:24
  163.6 2.5 %collective-permute-done.2 = f32[16,16]{1,0:T(8,128)S(1)} collective-permute-done((f32[16,16]{1,0:T(8,128)S(1)}, f32[16,16]{1,0:T(8,128)S(1)}, u32[]{:S(2)}, u32[]{:S(2)}) %collective-permute-start.2) | collective-permute-done | bytes 1056 | tf_op jit(solution)/shard_map/ppermute | solution.py:24
  166.4 15.2 %collective-permute-done.3 = f32[16,16]{1,0:T(8,128)S(1)} collective-permute-done((f32[16,16]{1,0:T(8,128)S(1)}, f32[16,16]{1,0:T(8,128)S(1)}, u32[]{:S(2)}, u32[]{:S(2)}) %collective-permute-start.3) | collective-permute-done | bytes 1056 | tf_op jit(solution)/shard_map/ppermute | solution.py:24
  181.6 1.4 collective-permute-start.4
  183.0 2.2 %collective-permute-done.4 = f32[16,16]{1,0:T(8,128)S(1)} collective-permute-done((f32[16,16]{1,0:T(8,128)S(1)}, f32[16,16]{1,0:T(8,128)S(1)}, u32[]{:S(2)}, u32[]{:S(2)}) %collective-permute-start.4) | collective-permute-done | bytes 1056 | tf_op jit(solution)/shard_map/ppermute | solution.py:24
  185.2 2.6 %collective-permute-start.5 = (f32[16,16]{1,0:T(8,128)S(1)}, f32[16,16]{1,0:T(8,128)S(1)}, u32[]{:S(2)}, u32[]{:S(2)}) collective-permute-start(f32[16,16]{1,0:T(8,128)S(1)} %add.57), channel_id=1, source_target_pairs={{0,8},{1,9},{2,10},{3,11},{4,12},{5,13},{6,14},{7,15},{8,0},{9,1},... | collective-permute-start | bytes 3080 | tf_op jit(solution)/shard_map/ppermute | solution.py:24
  187.9 1.3 collective-permute-start.1
  189.2 0.6 collective-permute-done.5
  189.8 1.2 select_add_fusion
  191.0 0.6 fusion.13
  194.1 1.3 copy-done
  195.3 4.4 %fusion.8 = f32[1,768,768]{2,1,0:T(8,128)} fusion(f32[768,768]{1,0:T(8,128)S(1)} %fusion.9, f32[768,768]{1,0:T(8,128)} %get-tuple-element.26, f32[768,768]{1,0:T(8,128)S(1)} %copy-done, f32[2,768,768]{2,1,0:T(8,128)} %get-tuple-element.24), kind=kLoop, calls=%fused_computation.15 | loop fusion | flops 1769472 | bytes 11796480 | tf_op jit(solution)/shard_map/broadcast_in_dim | solution.py:273
  (91 shorter events, 2.8 us)
Async XLA Ops:
  2.7 14.2 %copy-start.3 = (f32[3]{0:T(128)S(1)}, f32[3]{0:T(128)}, u32[]{:S(2)}) copy-start(f32[3]{0:T(128)} %param.8) | copy-start | bytes 40
  9.6 17.3 %all-to-all-start = ((f32[16,1,1536]{2,1,0:T(1,128)}), f32[16,1,1536]{2,1,0:T(1,128)S(1)}, u32[]{:S(2)}, u32[]{:S(2)}) async-start(f32[16,1,1536]{2,1,0:T(1,128)} %reshape.57), calls=%async_computation | async-start | bytes 196608 | tf_op jit(solution)/shard_map/all_to_all | solution.py:235
  20.8 3.4 %copy-start.4 = (s32[16]{0:T(128)S(1)}, s32[16]{0:T(128)}, u32[]{:S(2)}) copy-start(s32[16]{0:T(128)} %param.10) | copy-start | bytes 196
  47.5 144.2 %collective-permute-start = (f32[21,128,128]{2,1,0:T(8,128)S(1)}, f32[21,128,128]{2,1,0:T(8,128)S(1)}, u32[]{:S(2)}, u32[]{:S(2)}) collective-permute-start(f32[21,128,128]{2,1,0:T(8,128)S(1)} %constant_dynamic-update-slice_fusion), channel_id=1, source_target_pairs={{1,0},{2,1},{3,2},{4,3},{5,4},{6,5},{7,6},{8,7},{9,8},{10,9},{11,1... | collective-permute-start | bytes 4128776 | tf_op jit(solution)/shard_map/ppermute | solution.py:14
  48.8 117.3 %collective-permute-start.2 = (f32[16,16]{1,0:T(8,128)S(1)}, f32[16,16]{1,0:T(8,128)S(1)}, u32[]{:S(2)}, u32[]{:S(2)}) collective-permute-start(f32[16,16]{1,0:T(8,128)S(1)} %add.54), channel_id=1, source_target_pairs={{0,1},{1,0},{2,3},{3,2},{4,5},{5,4},{6,7},{7,6},{8,9},{9,8},{10,11... | collective-permute-start | bytes 3080 | tf_op jit(solution)/shard_map/ppermute | solution.py:24
  166.1 15.4 %collective-permute-start.3 = (f32[16,16]{1,0:T(8,128)S(1)}, f32[16,16]{1,0:T(8,128)S(1)}, u32[]{:S(2)}, u32[]{:S(2)}) collective-permute-start(f32[16,16]{1,0:T(8,128)S(1)} %add.55), channel_id=1, source_target_pairs={{0,2},{1,3},{2,0},{3,1},{4,6},{5,7},{6,4},{7,5},{8,10},{9,11},{10,... | collective-permute-start | bytes 3080 | tf_op jit(solution)/shard_map/ppermute | solution.py:24
  181.6 3.7 %collective-permute-start.4 = (f32[16,16]{1,0:T(8,128)S(1)}, f32[16,16]{1,0:T(8,128)S(1)}, u32[]{:S(2)}, u32[]{:S(2)}) collective-permute-start(f32[16,16]{1,0:T(8,128)S(1)} %add.56), channel_id=1, source_target_pairs={{0,4},{1,5},{2,6},{3,7},{4,0},{5,1},{6,2},{7,3},{8,12},{9,13},{10,... | collective-permute-start | bytes 3080 | tf_op jit(solution)/shard_map/ppermute | solution.py:24
  185.2 4.5 %collective-permute-start.5 = (f32[16,16]{1,0:T(8,128)S(1)}, f32[16,16]{1,0:T(8,128)S(1)}, u32[]{:S(2)}, u32[]{:S(2)}) collective-permute-start(f32[16,16]{1,0:T(8,128)S(1)} %add.57), channel_id=1, source_target_pairs={{0,8},{1,9},{2,10},{3,11},{4,12},{5,13},{6,14},{7,15},{8,0},{9,1},... | collective-permute-start | bytes 3080 | tf_op jit(solution)/shard_map/ppermute | solution.py:24
  187.9 3.2 %collective-permute-start.1 = (f32[16,768]{1,0:T(8,128)S(1)}, f32[16,768]{1,0:T(8,128)S(1)}, u32[]{:S(2)}, u32[]{:S(2)}) collective-permute-start(f32[16,768]{1,0:T(8,128)S(1)} %broadcast_select_fusion.1), channel_id=1, source_target_pairs={{1,0},{2,1},{3,2},{4,3},{5,4},{6,5},{7,6},{8,7},{9,8},{10,9},{11,1... | collective-permute-start | bytes 147464 | tf_op jit(solution)/shard_map/ppermute | solution.py:14
  193.7 1.7 copy-start

commit v6 on v5

--- a/solution.py
+++ b/solution.py
@@ -192,10 +192,10 @@
         hi = lo + block_size
         block_ref[...] = work_ref[lo:hi, lo:hi]
         sweep(block_ref)
-        solved = -exact_matmul(block_ref[...], work_ref[lo:hi, hi:])
+        solved = -split_matmul(block_ref[...], work_ref[lo:hi, hi:])
         solved_ref[lo:hi, :] = solved[:, mesh_width - hi :]
         if hi < mesh_width:
-            work_ref[hi:, hi:] = work_ref[hi:, hi:] - exact_matmul(work_ref[hi:, lo:hi], solved)
+            work_ref[hi:, hi:] = work_ref[hi:, hi:] - split_matmul(work_ref[hi:, lo:hi], solved)
 
 
 def eliminate(hessian, border, prior_diag, coupling_block):

time: 201 us -> 197 us (0.980)
  starting transfers between devices: 129 us -> 124 us
    ppermute x4, starting transfers between devices: 119 us -> 114 us  [butterfly_sum(): x = x + lax.ppermute(x, axis, pairs)]
where the time goes in v6:
time: 197 us; the launch traced here: 195 us
  starting transfers between devices  124 us (63%)
  waiting for transfers between devices  20.9 us (11%)
  other arithmetic  19.4 us (10%)
  Pallas kernels  13.4 us (7%)
  local copies, waits for them, and re-layouts  11.4 us (6%)
  between operations  5.9 us (3%)
    ppermute x4, starting transfers between devices, butterfly_sum(): x = x + lax.ppermute(x, axis, pairs)  114 us
    ppermute x4, waiting for transfers between devices, butterfly_sum(): x = x + lax.ppermute(x, axis, pairs)  20.9 us
    pallas_call x1, Pallas kernels, assemble(): pl.pallas_call(assemble_kernel, grid=(total_reads // chunk,), in_specs=[p...  13.4 us
    broadcast_in_dim x3, other arithmetic, local(): return (sep_block[None], fill[None], sep_border[None], tip)  8.38 us
    all_to_all x1, starting transfers between devices, local(): lax.all_to_all(packed, 'tm', split_axis=2, concat_axis=1, tiled=True)  7.39 us
    unnamed x71, local copies, waits for them, and re-layouts  7.11 us
    unnamed x2, other arithmetic  4.14 us
  transfers between devices with their start and end apart: 7, of which 4 were waited for; matrix products, arithmetic and copies ran while one was open for 4% of the time, Pallas kernels for 0%

profile of v6, /device:TPU:0, one launch (start us, length us, event | category | flops | bytes accessed | tf_op | source)
XLA Modules:
  0.0 195.4 jit_solution(10934220136456278975)
XLA Ops:
  0.6 0.7 convert_element_type.28
  1.4 0.3 copy.83
  1.7 1.0 copy.84
  2.7 1.0 copy.85
  3.8 2.2 %fusion.17 = f32[1024,1,24]{2,1,0:T(1,128)S(1)} fusion(f32[16,1,1024]{0,1,2:T(1,128)S(1)} %copy.85, f32[4,1,1024]{0,1,2:T(1,128)S(1)} %copy.84, f32[4,1,1024]{0,1,2:T(1,128)S(1)} %copy.83), kind=kLoop, calls=%fused_computation.118 | loop fusion | flops 49152 | bytes 196608
  6.0 0.6 broadcast.22
  6.6 1.9 reduce
  8.5 1.0 reshape.57
  9.6 7.4 %all-to-all-start = ((f32[16,1,1536]{2,1,0:T(1,128)}), f32[16,1,1536]{2,1,0:T(1,128)S(1)}, u32[]{:S(2)}, u32[]{:S(2)}) async-start(f32[16,1,1536]{2,1,0:T(1,128)} %reshape.57), calls=%async_computation | async-start | bytes 196608 | tf_op jit(solution)/shard_map/all_to_all | solution.py:235
  17.0 0.6 fusion.15
  20.8 3.4 %broadcast_multiply_fusion = (f32[768,768]{1,0:T(8,128)S(1)}, f32[768,768]{1,0:T(8,128)}) fusion(f32[768,768]{1,0:T(8,128)} %param.9, f32[]{:T(128)} %bitcast.9, f32[]{:T(128)} %bitcast.7), kind=kLoop, calls=%fused_computation.18 | loop fusion | flops 1179648 | bytes 7077896 | tf_op jit(solution)/shard_map/mul | solution.py:243
  24.2 0.6 dynamic_slice.7
  25.6 0.6 fusion.16
  26.8 0.9 reduce.1
  27.7 0.9 reshape.58
  28.9 13.4 %shard_map.93 = (f32[2,768,768]{2,1,0:T(8,128)}, f32[2,16,768]{2,1,0:T(8,128)S(1)}, f32[16,16]{1,0:T(8,128)S(1)}) custom-call(f32[1]{0:T(128)} %bitcast.4.end_ref, f32[24,1024]{1,0:T(8,128)S(1)} %bitcast.217), custom_call_target="tpu_custom_call" | custom-call | tf_op jit(solution)/shard_map/pallas_call | solution.py:114
  42.2 1.6 conditional.1
  42.3 1.6 broadcast.13
  43.8 3.4 %select_bitcast_fusion = (f32[1,768,768]{2,1,0:T(8,128)}, f32[768,768]{1,0:T(8,128)S(1)}) fusion(f32[768,768]{1,0:T(8,128)} %get-tuple-element.26, f32[768,768]{1,0:T(8,128)S(1)} %get-tuple-element.48, pred[]{:T(512)} %bitcast.8, pred[]{:T(512)S(6)} %gt.3), kind=kLoop, calls=%fused_computation.16 | loop fusion | flops 1769472 | bytes 9437186 | tf_op jit(solution)/shard_map/broadcast_in_dim | solution.py:273
  47.5 1.3 collective-permute-start
  48.8 110.5 %collective-permute-start.2 = (f32[16,16]{1,0:T(8,128)S(1)}, f32[16,16]{1,0:T(8,128)S(1)}, u32[]{:S(2)}, u32[]{:S(2)}) collective-permute-start(f32[16,16]{1,0:T(8,128)S(1)} %add.54), channel_id=1, source_target_pairs={{0,1},{1,0},{2,3},{3,2},{4,5},{5,4},{6,7},{7,6},{8,9},{9,8},{10,11... | collective-permute-start | bytes 3080 | tf_op jit(solution)/shard_map/ppermute | solution.py:24
  159.3 2.5 %collective-permute-done.2 = f32[16,16]{1,0:T(8,128)S(1)} collective-permute-done((f32[16,16]{1,0:T(8,128)S(1)}, f32[16,16]{1,0:T(8,128)S(1)}, u32[]{:S(2)}, u32[]{:S(2)}) %collective-permute-start.2) | collective-permute-done | bytes 1056 | tf_op jit(solution)/shard_map/ppermute | solution.py:24
  161.8 2.0 %collective-permute-start.3 = (f32[16,16]{1,0:T(8,128)S(1)}, f32[16,16]{1,0:T(8,128)S(1)}, u32[]{:S(2)}, u32[]{:S(2)}) collective-permute-start(f32[16,16]{1,0:T(8,128)S(1)} %add.55), channel_id=1, source_target_pairs={{0,2},{1,3},{2,0},{3,1},{4,6},{5,7},{6,4},{7,5},{8,10},{9,11},{10,... | collective-permute-start | bytes 3080 | tf_op jit(solution)/shard_map/ppermute | solution.py:24
  163.8 13.4 %collective-permute-done.3 = f32[16,16]{1,0:T(8,128)S(1)} collective-permute-done((f32[16,16]{1,0:T(8,128)S(1)}, f32[16,16]{1,0:T(8,128)S(1)}, u32[]{:S(2)}, u32[]{:S(2)}) %collective-permute-start.3) | collective-permute-done | bytes 1056 | tf_op jit(solution)/shard_map/ppermute | solution.py:24
  177.3 3.6 %collective-permute-done.4 = f32[16,16]{1,0:T(8,128)S(1)} collective-permute-done((f32[16,16]{1,0:T(8,128)S(1)}, f32[16,16]{1,0:T(8,128)S(1)}, u32[]{:S(2)}, u32[]{:S(2)}) %collective-permute-start.4) | collective-permute-done | bytes 1056 | tf_op jit(solution)/shard_map/ppermute | solution.py:24
  180.9 2.0 %collective-permute-start.5 = (f32[16,16]{1,0:T(8,128)S(1)}, f32[16,16]{1,0:T(8,128)S(1)}, u32[]{:S(2)}, u32[]{:S(2)}) collective-permute-start(f32[16,16]{1,0:T(8,128)S(1)} %add.57), channel_id=1, source_target_pairs={{0,8},{1,9},{2,10},{3,11},{4,12},{5,13},{6,14},{7,15},{8,0},{9,1},... | collective-permute-start | bytes 3080 | tf_op jit(solution)/shard_map/ppermute | solution.py:24
  182.9 1.3 collective-permute-start.1
  184.2 1.3 collective-permute-done.5
  185.5 1.2 select_add_fusion
  186.7 0.6 fusion.13
  189.8 1.3 copy-done
  191.0 4.4 %fusion.8 = f32[1,768,768]{2,1,0:T(8,128)} fusion(f32[768,768]{1,0:T(8,128)S(1)} %fusion.9, f32[768,768]{1,0:T(8,128)} %get-tuple-element.26, f32[768,768]{1,0:T(8,128)S(1)} %copy-done, f32[2,768,768]{2,1,0:T(8,128)} %get-tuple-element.24), kind=kLoop, calls=%fused_computation.15 | loop fusion | flops 1769472 | bytes 11796480 | tf_op jit(solution)/shard_map/broadcast_in_dim | solution.py:273
  (91 shorter events, 2.6 us)
Async XLA Ops:
  2.7 14.2 %copy-start.3 = (f32[3]{0:T(128)S(1)}, f32[3]{0:T(128)}, u32[]{:S(2)}) copy-start(f32[3]{0:T(128)} %param.8) | copy-start | bytes 40
  9.6 17.3 %all-to-all-start = ((f32[16,1,1536]{2,1,0:T(1,128)}), f32[16,1,1536]{2,1,0:T(1,128)S(1)}, u32[]{:S(2)}, u32[]{:S(2)}) async-start(f32[16,1,1536]{2,1,0:T(1,128)} %reshape.57), calls=%async_computation | async-start | bytes 196608 | tf_op jit(solution)/shard_map/all_to_all | solution.py:235
  20.8 3.4 %copy-start.4 = (s32[16]{0:T(128)S(1)}, s32[16]{0:T(128)}, u32[]{:S(2)}) copy-start(s32[16]{0:T(128)} %param.10) | copy-start | bytes 196
  47.5 139.8 %collective-permute-start = (f32[21,128,128]{2,1,0:T(8,128)S(1)}, f32[21,128,128]{2,1,0:T(8,128)S(1)}, u32[]{:S(2)}, u32[]{:S(2)}) collective-permute-start(f32[21,128,128]{2,1,0:T(8,128)S(1)} %constant_dynamic-update-slice_fusion), channel_id=1, source_target_pairs={{1,0},{2,1},{3,2},{4,3},{5,4},{6,5},{7,6},{8,7},{9,8},{10,9},{11,1... | collective-permute-start | bytes 4128776 | tf_op jit(solution)/shard_map/ppermute | solution.py:14
  48.8 113.0 %collective-permute-start.2 = (f32[16,16]{1,0:T(8,128)S(1)}, f32[16,16]{1,0:T(8,128)S(1)}, u32[]{:S(2)}, u32[]{:S(2)}) collective-permute-start(f32[16,16]{1,0:T(8,128)S(1)} %add.54), channel_id=1, source_target_pairs={{0,1},{1,0},{2,3},{3,2},{4,5},{5,4},{6,7},{7,6},{8,9},{9,8},{10,11... | collective-permute-start | bytes 3080 | tf_op jit(solution)/shard_map/ppermute | solution.py:24
  161.8 15.4 %collective-permute-start.3 = (f32[16,16]{1,0:T(8,128)S(1)}, f32[16,16]{1,0:T(8,128)S(1)}, u32[]{:S(2)}, u32[]{:S(2)}) collective-permute-start(f32[16,16]{1,0:T(8,128)S(1)} %add.55), channel_id=1, source_target_pairs={{0,2},{1,3},{2,0},{3,1},{4,6},{5,7},{6,4},{7,5},{8,10},{9,11},{10,... | collective-permute-start | bytes 3080 | tf_op jit(solution)/shard_map/ppermute | solution.py:24
  177.3 3.7 %collective-permute-start.4 = (f32[16,16]{1,0:T(8,128)S(1)}, f32[16,16]{1,0:T(8,128)S(1)}, u32[]{:S(2)}, u32[]{:S(2)}) collective-permute-start(f32[16,16]{1,0:T(8,128)S(1)} %add.56), channel_id=1, source_target_pairs={{0,4},{1,5},{2,6},{3,7},{4,0},{5,1},{6,2},{7,3},{8,12},{9,13},{10,... | collective-permute-start | bytes 3080 | tf_op jit(solution)/shard_map/ppermute | solution.py:24
  180.9 4.5 %collective-permute-start.5 = (f32[16,16]{1,0:T(8,128)S(1)}, f32[16,16]{1,0:T(8,128)S(1)}, u32[]{:S(2)}, u32[]{:S(2)}) collective-permute-start(f32[16,16]{1,0:T(8,128)S(1)} %add.57), channel_id=1, source_target_pairs={{0,8},{1,9},{2,10},{3,11},{4,12},{5,13},{6,14},{7,15},{8,0},{9,1},... | collective-permute-start | bytes 3080 | tf_op jit(solution)/shard_map/ppermute | solution.py:24
  182.9 3.8 %collective-permute-start.1 = (f32[16,768]{1,0:T(8,128)S(1)}, f32[16,768]{1,0:T(8,128)S(1)}, u32[]{:S(2)}, u32[]{:S(2)}) collective-permute-start(f32[16,768]{1,0:T(8,128)S(1)} %broadcast_select_fusion.1), channel_id=1, source_target_pairs={{1,0},{2,1},{3,2},{4,3},{5,4},{6,5},{7,6},{8,7},{9,8},{10,9},{11,1... | collective-permute-start | bytes 147464 | tf_op jit(solution)/shard_map/ppermute | solution.py:14
  189.4 1.7 copy-start

commit v7 on v6

--- a/solution.py
+++ b/solution.py
@@ -18,11 +18,12 @@
     length = lax.axis_size(axis)
     if length & (length - 1):
         return lax.psum(x, axis)
-    stride = 1
-    while stride < length:
+    strides = [1]
+    while strides[-1] * 2 < length:
+        strides.append(strides[-1] * 2)
+    for stride in [1] + strides[:0:-1]:
         pairs = [(i, i ^ stride) for i in range(length)]
         x = x + lax.ppermute(x, axis, pairs)
-        stride *= 2
     return x
 
 

time: 197 us -> 198 us (level)
  waiting for transfers between devices: 20.9 us -> 23 us
    ppermute x4, waiting for transfers between devices: 20.9 us -> 23 us  [butterfly_sum(): x = x + lax.ppermute(x, axis, pairs)]
where the time goes in v7:
time: 198 us; the launch traced here: 197 us
  starting transfers between devices  124 us (63%)
  waiting for transfers between devices  23 us (12%)
  other arithmetic  19.4 us (10%)
  Pallas kernels  13.4 us (7%)
  local copies, waits for them, and re-layouts  11.4 us (6%)
  between operations  5.9 us (3%)
    ppermute x4, starting transfers between devices, butterfly_sum(): x = x + lax.ppermute(x, axis, pairs)  114 us
    ppermute x4, waiting for transfers between devices, butterfly_sum(): x = x + lax.ppermute(x, axis, pairs)  23 us
    pallas_call x1, Pallas kernels, assemble(): pl.pallas_call(assemble_kernel, grid=(total_reads // chunk,), in_specs=[p...  13.4 us
    broadcast_in_dim x3, other arithmetic, local(): return (sep_block[None], fill[None], sep_border[None], tip)  8.38 us
    all_to_all x1, starting transfers between devices, local(): lax.all_to_all(packed, 'tm', split_axis=2, concat_axis=1, tiled=True)  7.39 us
    unnamed x71, local copies, waits for them, and re-layouts  7.11 us
    unnamed x2, other arithmetic  4.14 us
  transfers between devices with their start and end apart: 7, of which 4 were waited for; matrix products, arithmetic and copies ran while one was open for 4% of the time, Pallas kernels for 0%

profile of v7, /device:TPU:0, one launch (start us, length us, event | category | flops | bytes accessed | tf_op | source)
XLA Modules:
  0.0 196.7 jit_solution(17350085847045503174)
XLA Ops:
  0.6 0.7 convert_element_type.28
  1.4 0.3 copy.83
  1.7 1.0 copy.84
  2.7 1.0 copy.85
  3.8 2.2 %fusion.17 = f32[1024,1,24]{2,1,0:T(1,128)S(1)} fusion(f32[16,1,1024]{0,1,2:T(1,128)S(1)} %copy.85, f32[4,1,1024]{0,1,2:T(1,128)S(1)} %copy.84, f32[4,1,1024]{0,1,2:T(1,128)S(1)} %copy.83), kind=kLoop, calls=%fused_computation.118 | loop fusion | flops 49152 | bytes 196608
  6.0 0.6 broadcast.22
  6.6 1.9 reduce
  8.5 1.0 reshape.57
  9.6 7.4 %all-to-all-start = ((f32[16,1,1536]{2,1,0:T(1,128)}), f32[16,1,1536]{2,1,0:T(1,128)S(1)}, u32[]{:S(2)}, u32[]{:S(2)}) async-start(f32[16,1,1536]{2,1,0:T(1,128)} %reshape.57), calls=%async_computation | async-start | bytes 196608 | tf_op jit(solution)/shard_map/all_to_all | solution.py:236
  17.0 0.6 fusion.15
  20.8 3.4 %broadcast_multiply_fusion = (f32[768,768]{1,0:T(8,128)S(1)}, f32[768,768]{1,0:T(8,128)}) fusion(f32[768,768]{1,0:T(8,128)} %param.9, f32[]{:T(128)} %bitcast.9, f32[]{:T(128)} %bitcast.7), kind=kLoop, calls=%fused_computation.18 | loop fusion | flops 1179648 | bytes 7077896 | tf_op jit(solution)/shard_map/mul | solution.py:244
  24.2 0.6 dynamic_slice.7
  25.6 0.6 fusion.16
  26.8 0.9 reduce.1
  27.7 0.9 reshape.58
  28.9 13.4 %shard_map.93 = (f32[2,768,768]{2,1,0:T(8,128)}, f32[2,16,768]{2,1,0:T(8,128)S(1)}, f32[16,16]{1,0:T(8,128)S(1)}) custom-call(f32[1]{0:T(128)} %bitcast.4.end_ref, f32[24,1024]{1,0:T(8,128)S(1)} %bitcast.217), custom_call_target="tpu_custom_call" | custom-call | tf_op jit(solution)/shard_map/pallas_call | solution.py:115
  42.2 1.6 conditional.1
  42.3 1.6 broadcast.13
  43.8 3.4 %select_bitcast_fusion = (f32[1,768,768]{2,1,0:T(8,128)}, f32[768,768]{1,0:T(8,128)S(1)}) fusion(f32[768,768]{1,0:T(8,128)} %get-tuple-element.26, f32[768,768]{1,0:T(8,128)S(1)} %get-tuple-element.48, pred[]{:T(512)} %bitcast.8, pred[]{:T(512)S(6)} %gt.3), kind=kLoop, calls=%fused_computation.16 | loop fusion | flops 1769472 | bytes 9437186 | tf_op jit(solution)/shard_map/broadcast_in_dim | solution.py:274
  47.5 1.3 collective-permute-start
  48.8 1.2 collective-permute-start.2
  50.0 2.5 %collective-permute-done.2 = f32[16,16]{1,0:T(8,128)S(1)} collective-permute-done((f32[16,16]{1,0:T(8,128)S(1)}, f32[16,16]{1,0:T(8,128)S(1)}, u32[]{:S(2)}, u32[]{:S(2)}) %collective-permute-start.2) | collective-permute-done | bytes 1056 | tf_op jit(solution)/shard_map/ppermute | solution.py:26
  52.5 112.2 %collective-permute-start.3 = (f32[16,16]{1,0:T(8,128)S(1)}, f32[16,16]{1,0:T(8,128)S(1)}, u32[]{:S(2)}, u32[]{:S(2)}) collective-permute-start(f32[16,16]{1,0:T(8,128)S(1)} %add.55), channel_id=1, source_target_pairs={{0,8},{1,9},{2,10},{3,11},{4,12},{5,13},{6,14},{7,15},{8,0},{9,1},... | collective-permute-start | bytes 3080 | tf_op jit(solution)/shard_map/ppermute | solution.py:26
  164.7 14.7 %collective-permute-done.3 = f32[16,16]{1,0:T(8,128)S(1)} collective-permute-done((f32[16,16]{1,0:T(8,128)S(1)}, f32[16,16]{1,0:T(8,128)S(1)}, u32[]{:S(2)}, u32[]{:S(2)}) %collective-permute-start.3) | collective-permute-done | bytes 1056 | tf_op jit(solution)/shard_map/ppermute | solution.py:26
  179.5 0.3 collective-permute-start.4
  179.7 3.4 %collective-permute-done.4 = f32[16,16]{1,0:T(8,128)S(1)} collective-permute-done((f32[16,16]{1,0:T(8,128)S(1)}, f32[16,16]{1,0:T(8,128)S(1)}, u32[]{:S(2)}, u32[]{:S(2)}) %collective-permute-start.4) | collective-permute-done | bytes 1056 | tf_op jit(solution)/shard_map/ppermute | solution.py:26
  183.1 1.3 collective-permute-start.1
  184.4 2.3 %collective-permute-done.5 = f32[16,16]{1,0:T(8,128)S(1)} collective-permute-done((f32[16,16]{1,0:T(8,128)S(1)}, f32[16,16]{1,0:T(8,128)S(1)}, u32[]{:S(2)}, u32[]{:S(2)}) %collective-permute-start.5) | collective-permute-done | bytes 1056 | tf_op jit(solution)/shard_map/ppermute | solution.py:26
  186.8 1.2 select_add_fusion
  188.0 0.6 fusion.13
  191.0 1.3 copy-done
  192.3 4.4 %fusion.8 = f32[1,768,768]{2,1,0:T(8,128)} fusion(f32[768,768]{1,0:T(8,128)S(1)} %fusion.9, f32[768,768]{1,0:T(8,128)} %get-tuple-element.26, f32[768,768]{1,0:T(8,128)S(1)} %copy-done, f32[2,768,768]{2,1,0:T(8,128)} %get-tuple-element.24), kind=kLoop, calls=%fused_computation.15 | loop fusion | flops 1769472 | bytes 11796480 | tf_op jit(solution)/shard_map/broadcast_in_dim | solution.py:274
  (91 shorter events, 2.6 us)
Async XLA Ops:
  2.7 14.2 %copy-start.3 = (f32[3]{0:T(128)S(1)}, f32[3]{0:T(128)}, u32[]{:S(2)}) copy-start(f32[3]{0:T(128)} %param.8) | copy-start | bytes 40
  9.6 17.3 %all-to-all-start = ((f32[16,1,1536]{2,1,0:T(1,128)}), f32[16,1,1536]{2,1,0:T(1,128)S(1)}, u32[]{:S(2)}, u32[]{:S(2)}) async-start(f32[16,1,1536]{2,1,0:T(1,128)} %reshape.57), calls=%async_computation | async-start | bytes 196608 | tf_op jit(solution)/shard_map/all_to_all | solution.py:236
  20.8 3.4 %copy-start.4 = (s32[16]{0:T(128)S(1)}, s32[16]{0:T(128)}, u32[]{:S(2)}) copy-start(s32[16]{0:T(128)} %param.10) | copy-start | bytes 196
  47.5 141.1 %collective-permute-start = (f32[21,128,128]{2,1,0:T(8,128)S(1)}, f32[21,128,128]{2,1,0:T(8,128)S(1)}, u32[]{:S(2)}, u32[]{:S(2)}) collective-permute-start(f32[21,128,128]{2,1,0:T(8,128)S(1)} %constant_dynamic-update-slice_fusion), channel_id=1, source_target_pairs={{1,0},{2,1},{3,2},{4,3},{5,4},{6,5},{7,6},{8,7},{9,8},{10,9},{11,1... | collective-permute-start | bytes 4128776 | tf_op jit(solution)/shard_map/ppermute | solution.py:14
  48.8 3.7 %collective-permute-start.2 = (f32[16,16]{1,0:T(8,128)S(1)}, f32[16,16]{1,0:T(8,128)S(1)}, u32[]{:S(2)}, u32[]{:S(2)}) collective-permute-start(f32[16,16]{1,0:T(8,128)S(1)} %add.54), channel_id=1, source_target_pairs={{0,1},{1,0},{2,3},{3,2},{4,5},{5,4},{6,7},{7,6},{8,9},{9,8},{10,11... | collective-permute-start | bytes 3080 | tf_op jit(solution)/shard_map/ppermute | solution.py:26
  52.5 126.9 %collective-permute-start.3 = (f32[16,16]{1,0:T(8,128)S(1)}, f32[16,16]{1,0:T(8,128)S(1)}, u32[]{:S(2)}, u32[]{:S(2)}) collective-permute-start(f32[16,16]{1,0:T(8,128)S(1)} %add.55), channel_id=1, source_target_pairs={{0,8},{1,9},{2,10},{3,11},{4,12},{5,13},{6,14},{7,15},{8,0},{9,1},... | collective-permute-start | bytes 3080 | tf_op jit(solution)/shard_map/ppermute | solution.py:26
  179.5 3.7 %collective-permute-start.4 = (f32[16,16]{1,0:T(8,128)S(1)}, f32[16,16]{1,0:T(8,128)S(1)}, u32[]{:S(2)}, u32[]{:S(2)}) collective-permute-start(f32[16,16]{1,0:T(8,128)S(1)} %add.56), channel_id=1, source_target_pairs={{0,4},{1,5},{2,6},{3,7},{4,0},{5,1},{6,2},{7,3},{8,12},{9,13},{10,... | collective-permute-start | bytes 3080 | tf_op jit(solution)/shard_map/ppermute | solution.py:26
  183.1 3.7 %collective-permute-start.5 = (f32[16,16]{1,0:T(8,128)S(1)}, f32[16,16]{1,0:T(8,128)S(1)}, u32[]{:S(2)}, u32[]{:S(2)}) collective-permute-start(f32[16,16]{1,0:T(8,128)S(1)} %add.57), channel_id=1, source_target_pairs={{0,2},{1,3},{2,0},{3,1},{4,6},{5,7},{6,4},{7,5},{8,10},{9,11},{10,... | collective-permute-start | bytes 3080 | tf_op jit(solution)/shard_map/ppermute | solution.py:26
  183.1 4.9 %collective-permute-start.1 = (f32[16,768]{1,0:T(8,128)S(1)}, f32[16,768]{1,0:T(8,128)S(1)}, u32[]{:S(2)}, u32[]{:S(2)}) collective-permute-start(f32[16,768]{1,0:T(8,128)S(1)} %broadcast_select_fusion.1), channel_id=1, source_target_pairs={{1,0},{2,1},{3,2},{4,3},{5,4},{6,5},{7,6},{8,7},{9,8},{10,9},{11,1... | collective-permute-start | bytes 147464 | tf_op jit(solution)/shard_map/ppermute | solution.py:14
  190.7 1.7 copy-start

commit v8 on v6

--- a/solution.py
+++ b/solution.py
@@ -166,9 +166,8 @@
     sub = lax.broadcasted_iota(jnp.int32, (size, size), 0)
     lane_row = lax.broadcasted_iota(jnp.int32, (1, size), 1)
 
-    def body(k, carry):
-        current = block_ref[...]
-        row = block_ref[pl.ds(k, 1), :]
+    def body(k, current):
+        row = jnp.sum(jnp.where(sub == k, current, 0.0), axis=0, keepdims=True)
         col = jnp.sum(jnp.where(lane == k, current, 0.0), axis=1, keepdims=True)
         pivot = jnp.sum(jnp.where(lane_row == k, row, 0.0), axis=1, keepdims=True)
         inverse = 1.0 / pivot
@@ -176,11 +175,9 @@
         update = current - col * scaled_row
         update = jnp.where(sub == k, scaled_row, update)
         update = jnp.where(lane == k, col * inverse, update)
-        update = jnp.where((sub == k) & (lane == k), -inverse, update)
-        block_ref[...] = update
-        return carry
-
-    lax.fori_loop(0, size, body, 0)
+        return jnp.where((sub == k) & (lane == k), -inverse, update)
+
+    block_ref[...] = lax.fori_loop(0, size, body, block_ref[...])
 
 
 def eliminate_kernel(start_ref, work_ref, solved_ref, block_ref):

time: 197 us -> 211 us (1.071)
  Pallas kernels: 13.4 us -> 123 us
  starting transfers between devices: 124 us -> 28.5 us
  waiting for transfers between devices: 20.9 us -> 6.83 us
  matrix products: 0 us -> 7.26 us
  other arithmetic: 19.4 us -> 24.7 us
    pallas_call x0 -> x1, Pallas kernels: none -> 110 us  [eliminate(): pl.pallas_call(eliminate_kernel, out_shape=[jax.ShapeDtypeStruct((mesh_wi...]
    ppermute x4, starting transfers between devices: 114 us -> 18.5 us  [butterfly_sum(): x = x + lax.ppermute(x, axis, pairs)]
    ppermute x4, waiting for transfers between devices: 20.9 us -> 6.82 us  [butterfly_sum(): x = x + lax.ppermute(x, axis, pairs)]
    dot_general x0 -> x3, matrix products: none -> 7.26 us  [contract_rows(): lax.dot_general(left, right, (((0,), (0,)), ((), ())), preferred_element_...]
    add x0 -> x1, other arithmetic: none -> 2.67 us  [eliminate(): interior = hessian[1] + prior_diag]
    concatenate x0 -> x1, other arithmetic: none -> 2.6 us  [eliminate(): start = jnp.concatenate([interior, coupling_block, border[1].T], axis=1)]
  transfers between devices with their start and end apart: 7 -> 7, of which waited for: 4 -> 4; matrix products, arithmetic and copies ran while one was open for 4% -> 3% of each run, Pallas kernels for 0% -> 0%
where the time goes in v8:
time: 211 us; the launch traced here: 209 us
  Pallas kernels  123 us (58%)
  starting transfers between devices  28.5 us (14%)
  other arithmetic  24.7 us (12%)
  local copies, waits for them, and re-layouts  12.5 us (6%)
  matrix products  7.26 us (3%)
  waiting for transfers between devices  6.83 us (3%)
  between operations  5.9 us (3%)
    pallas_call x1, Pallas kernels, eliminate(): pl.pallas_call(eliminate_kernel, out_shape=[jax.ShapeDtypeStruct((mesh_wi...  110 us
    ppermute x4, starting transfers between devices, butterfly_sum(): x = x + lax.ppermute(x, axis, pairs)  18.5 us
    pallas_call x1, Pallas kernels, assemble(): pl.pallas_call(assemble_kernel, grid=(total_reads // chunk,), in_specs=[p...  13.4 us
    broadcast_in_dim x3, other arithmetic, local(): return (sep_block[None], fill[None], sep_border[None], tip)  8.38 us
    all_to_all x1, starting transfers between devices, local(): lax.all_to_all(packed, 'tm', split_axis=2, concat_axis=1, tiled=True)  7.39 us
    dot_general x3, matrix products, contract_rows(): lax.dot_general(left, right, (((0,), (0,)), ((), ())), preferred_element_...  7.26 us
    unnamed x71, local copies, waits for them, and re-layouts  7.11 us
    ppermute x4, waiting for transfers between devices, butterfly_sum(): x = x + lax.ppermute(x, axis, pairs)  6.82 us
  transfers between devices with their start and end apart: 7, of which 4 were waited for; matrix products, arithmetic and copies ran while one was open for 3% of the time, Pallas kernels for 0%

profile of v8, /device:TPU:0, one launch (start us, length us, event | category | flops | bytes accessed | tf_op | source)
XLA Modules:
  0.0 209.1 jit_solution(8518334507025484561)
XLA Ops:
  0.6 0.7 convert_element_type.28
  1.7 1.0 copy.84
  2.7 1.0 copy.85
  3.8 2.2 %fusion.17 = f32[1024,1,24]{2,1,0:T(1,128)S(1)} fusion(f32[16,1,1024]{0,1,2:T(1,128)S(1)} %copy.85, f32[4,1,1024]{0,1,2:T(1,128)S(1)} %copy.84, f32[4,1,1024]{0,1,2:T(1,128)S(1)} %copy.83), kind=kLoop, calls=%fused_computation.118 | loop fusion | flops 49152 | bytes 196608
  6.6 1.9 reduce
  8.5 1.0 reshape.57
  9.6 7.4 %all-to-all-start = ((f32[16,1,1536]{2,1,0:T(1,128)}), f32[16,1,1536]{2,1,0:T(1,128)S(1)}, u32[]{:S(2)}, u32[]{:S(2)}) async-start(f32[16,1,1536]{2,1,0:T(1,128)} %reshape.57), calls=%async_computation | async-start | bytes 196608 | tf_op jit(solution)/shard_map/all_to_all | solution.py:232
  20.8 3.4 %broadcast_multiply_fusion = (f32[768,768]{1,0:T(8,128)S(1)}, f32[768,768]{1,0:T(8,128)}) fusion(f32[768,768]{1,0:T(8,128)} %param.9, f32[]{:T(128)} %bitcast.9, f32[]{:T(128)} %bitcast.7), kind=kLoop, calls=%fused_computation.18 | loop fusion | flops 1179648 | bytes 7077896 | tf_op jit(solution)/shard_map/mul | solution.py:240
  26.8 0.9 reduce.1
  27.7 0.9 reshape.58
  28.9 13.4 %shard_map.93 = (f32[2,768,768]{2,1,0:T(8,128)}, f32[2,16,768]{2,1,0:T(8,128)S(1)}, f32[16,16]{1,0:T(8,128)S(1)}) custom-call(f32[1]{0:T(128)} %bitcast.4.end_ref, f32[24,1024]{1,0:T(8,128)S(1)} %bitcast.217), custom_call_target="tpu_custom_call" | custom-call | tf_op jit(solution)/shard_map/pallas_call | solution.py:114
  42.2 125.3 %conditional.1 = (f32[768,768]{1,0:T(8,128)}, f32[16,768]{1,0:T(8,128)S(1)}, f32[16,16]{1,0:T(8,128)S(1)}) conditional(s32[]{:T(128)} %convert_element_type.29, () %tuple.16, (f32[2,768,768]{2,1,0:T(8,128)}, f32[768,768]{1,0:T(8,128)}, f32[2,16,768]{2,1,0:T(8,128)S(1)}, f32[768,768]{1,0:T(8,128)S(1)}) %tuple.17), branch_computations={%region_1.2_spmd, %region_2.3_spmd} | conditional | flops 2845582080 | bytes 79942736 | solution.py:256
  42.5 2.7 %bitcast_add_fusion = f32[768,768]{1,0:T(8,128)S(1)} fusion(f32[768,768]{1,0:T(8,128)} %get-tuple-element.9, f32[2,768,768]{2,1,0:T(8,128)} %get-tuple-element.8), kind=kLoop, calls=%fused_computation.8 | loop fusion | flops 589824 | bytes 7077888 | tf_op jit(solution)/shard_map/cond/branch_1_fun/add | solution.py:201
  45.2 2.6 %pad_maximum_fusion.start_ref = f32[768,1552]{1,0:T(8,128)} fusion(f32[768,16]{1,0:T(8,128)S(1)} %slice_bitcast_fusion, f32[768,768]{1,0:T(8,128)S(1)} %get-tuple-element.10, f32[768,768]{1,0:T(8,128)S(1)} %bitcast_add_fusion), kind=kLoop, calls=%fused_computation | loop fusion | flops 2383872 | bytes 9535488 | tf_op jit(solution)/shard_map/cond/branch_1_fun/concatenate | solution.py:202
  47.8 110.1 %branch_1_fun.1 = (f32[768,1552]{1,0:T(8,128)}, f32[768,784]{1,0:T(8,128)}) custom-call(f32[768,1552]{1,0:T(8,128)} %pad_maximum_fusion.start_ref), custom_call_target="tpu_custom_call" | custom-call | tf_op jit(solution)/shard_map/cond/branch_1_fun/pallas_call | solution.py:204
  157.9 4.2 %fusion.2 = f32[784,784]{1,0:T(8,128)S(1)} fusion(f32[768,784]{1,0:T(8,128)} %get-tuple-element.13, f32[768,1552]{1,0:T(8,128)} %get-tuple-element.12), kind=kOutput, calls=%fused_computation.9 | convolution fusion | flops 947122176 | bytes 7963648 | tf_op jit(solution)/shard_map/cond/branch_1_fun/dot_general | solution.py:62
  162.8 1.5 fusion.5
  164.3 1.6 add_negate_fusion
  165.9 1.6 slice.222
  167.5 3.4 %select_bitcast_fusion = (f32[1,768,768]{2,1,0:T(8,128)}, f32[768,768]{1,0:T(8,128)S(1)}) fusion(f32[768,768]{1,0:T(8,128)} %get-tuple-element.26, f32[768,768]{1,0:T(8,128)S(1)} %get-tuple-element.48, pred[]{:T(512)} %bitcast.8, pred[]{:T(512)S(6)} %gt.3), kind=kLoop, calls=%fused_computation.16 | loop fusion | flops 1769472 | bytes 9437186 | tf_op jit(solution)/shard_map/broadcast_in_dim | solution.py:270
  171.2 1.3 collective-permute-start
  172.5 1.2 collective-permute-start.2
  173.7 2.5 %collective-permute-done.2 = f32[16,16]{1,0:T(8,128)S(1)} collective-permute-done((f32[16,16]{1,0:T(8,128)S(1)}, f32[16,16]{1,0:T(8,128)S(1)}, u32[]{:S(2)}, u32[]{:S(2)}) %collective-permute-start.2) | collective-permute-done | bytes 1056 | tf_op jit(solution)/shard_map/ppermute | solution.py:24
  176.3 1.6 collective-permute-start.3
  177.8 2.1 collective-permute-done.3
  179.9 13.1 %collective-permute-start.4 = (f32[16,16]{1,0:T(8,128)S(1)}, f32[16,16]{1,0:T(8,128)S(1)}, u32[]{:S(2)}, u32[]{:S(2)}) collective-permute-start(f32[16,16]{1,0:T(8,128)S(1)} %add.56), channel_id=1, source_target_pairs={{0,4},{1,5},{2,6},{3,7},{4,0},{5,1},{6,2},{7,3},{8,12},{9,13},{10,... | collective-permute-start | bytes 3080 | tf_op jit(solution)/shard_map/ppermute | solution.py:24
  193.0 1.6 collective-permute-done.4
  194.6 2.7 %collective-permute-start.5 = (f32[16,16]{1,0:T(8,128)S(1)}, f32[16,16]{1,0:T(8,128)S(1)}, u32[]{:S(2)}, u32[]{:S(2)}) collective-permute-start(f32[16,16]{1,0:T(8,128)S(1)} %add.57), channel_id=1, source_target_pairs={{0,8},{1,9},{2,10},{3,11},{4,12},{5,13},{6,14},{7,15},{8,0},{9,1},... | collective-permute-start | bytes 3080 | tf_op jit(solution)/shard_map/ppermute | solution.py:24
  197.3 1.3 collective-permute-start.1
  199.2 1.2 select_add_fusion
  203.4 1.3 copy-done
  204.7 4.4 %fusion.8 = f32[1,768,768]{2,1,0:T(8,128)} fusion(f32[768,768]{1,0:T(8,128)S(1)} %fusion.9, f32[768,768]{1,0:T(8,128)} %get-tuple-element.26, f32[768,768]{1,0:T(8,128)S(1)} %copy-done, f32[2,768,768]{2,1,0:T(8,128)} %get-tuple-element.24), kind=kLoop, calls=%fused_computation.15 | loop fusion | flops 1769472 | bytes 11796480 | tf_op jit(solution)/shard_map/broadcast_in_dim | solution.py:270
  (103 shorter events, 7.5 us)
Async XLA Ops:
  2.7 14.2 %copy-start.3 = (f32[3]{0:T(128)S(1)}, f32[3]{0:T(128)}, u32[]{:S(2)}) copy-start(f32[3]{0:T(128)} %param.8) | copy-start | bytes 40
  9.6 17.3 %all-to-all-start = ((f32[16,1,1536]{2,1,0:T(1,128)}), f32[16,1,1536]{2,1,0:T(1,128)S(1)}, u32[]{:S(2)}, u32[]{:S(2)}) async-start(f32[16,1,1536]{2,1,0:T(1,128)} %reshape.57), calls=%async_computation | async-start | bytes 196608 | tf_op jit(solution)/shard_map/all_to_all | solution.py:232
  20.8 3.4 %copy-start.4 = (s32[16]{0:T(128)S(1)}, s32[16]{0:T(128)}, u32[]{:S(2)}) copy-start(s32[16]{0:T(128)} %param.10) | copy-start | bytes 196
  157.9 4.2 %copy-start.1 = (f32[768,784]{1,0:T(8,128)S(1)}, f32[768,784]{1,0:T(8,128)}, u32[]{:S(2)}) copy-start(f32[768,784]{1,0:T(8,128)} %get-tuple-element.13) | copy-start | bytes 7225348 | tf_op jit(solution)/shard_map/cond
  157.9 4.9 %copy-start.2 = (f32[768,1552]{1,0:T(8,128)S(1)}, f32[768,1552]{1,0:T(8,128)}, u32[]{:S(2)}) copy-start(f32[768,1552]{1,0:T(8,128)} %get-tuple-element.12) | copy-start | bytes 14303236 | tf_op jit(solution)/shard_map/cond
  171.2 29.8 %collective-permute-start = (f32[21,128,128]{2,1,0:T(8,128)S(1)}, f32[21,128,128]{2,1,0:T(8,128)S(1)}, u32[]{:S(2)}, u32[]{:S(2)}) collective-permute-start(f32[21,128,128]{2,1,0:T(8,128)S(1)} %constant_dynamic-update-slice_fusion), channel_id=1, source_target_pairs={{1,0},{2,1},{3,2},{4,3},{5,4},{6,5},{7,6},{8,7},{9,8},{10,9},{11,1... | collective-permute-start | bytes 4128776 | tf_op jit(solution)/shard_map/ppermute | solution.py:14
  172.5 3.7 %collective-permute-start.2 = (f32[16,16]{1,0:T(8,128)S(1)}, f32[16,16]{1,0:T(8,128)S(1)}, u32[]{:S(2)}, u32[]{:S(2)}) collective-permute-start(f32[16,16]{1,0:T(8,128)S(1)} %add.54), channel_id=1, source_target_pairs={{0,1},{1,0},{2,3},{3,2},{4,5},{5,4},{6,7},{7,6},{8,9},{9,8},{10,11... | collective-permute-start | bytes 3080 | tf_op jit(solution)/shard_map/ppermute | solution.py:24
  176.3 3.7 %collective-permute-start.3 = (f32[16,16]{1,0:T(8,128)S(1)}, f32[16,16]{1,0:T(8,128)S(1)}, u32[]{:S(2)}, u32[]{:S(2)}) collective-permute-start(f32[16,16]{1,0:T(8,128)S(1)} %add.55), channel_id=1, source_target_pairs={{0,2},{1,3},{2,0},{3,1},{4,6},{5,7},{6,4},{7,5},{8,10},{9,11},{10,... | collective-permute-start | bytes 3080 | tf_op jit(solution)/shard_map/ppermute | solution.py:24
  179.9 14.7 %collective-permute-start.4 = (f32[16,16]{1,0:T(8,128)S(1)}, f32[16,16]{1,0:T(8,128)S(1)}, u32[]{:S(2)}, u32[]{:S(2)}) collective-permute-start(f32[16,16]{1,0:T(8,128)S(1)} %add.56), channel_id=1, source_target_pairs={{0,4},{1,5},{2,6},{3,7},{4,0},{5,1},{6,2},{7,3},{8,12},{9,13},{10,... | collective-permute-start | bytes 3080 | tf_op jit(solution)/shard_map/ppermute | solution.py:24
  194.6 4.5 %collective-permute-start.5 = (f32[16,16]{1,0:T(8,128)S(1)}, f32[16,16]{1,0:T(8,128)S(1)}, u32[]{:S(2)}, u32[]{:S(2)}) collective-permute-start(f32[16,16]{1,0:T(8,128)S(1)} %add.57), channel_id=1, source_target_pairs={{0,8},{1,9},{2,10},{3,11},{4,12},{5,13},{6,14},{7,15},{8,0},{9,1},... | collective-permute-start | bytes 3080 | tf_op jit(solution)/shard_map/ppermute | solution.py:24
  197.3 3.1 %collective-permute-start.1 = (f32[16,768]{1,0:T(8,128)S(1)}, f32[16,768]{1,0:T(8,128)S(1)}, u32[]{:S(2)}, u32[]{:S(2)}) collective-permute-start(f32[16,768]{1,0:T(8,128)S(1)} %broadcast_select_fusion.1), channel_id=1, source_target_pairs={{1,0},{2,1},{3,2},{4,3},{5,4},{6,5},{7,6},{8,7},{9,8},{10,9},{11,1... | collective-permute-start | bytes 147464 | tf_op jit(solution)/shard_map/ppermute | solution.py:14
  203.0 1.7 copy-start

commit v9 on v6

--- a/solution.py
+++ b/solution.py
@@ -109,7 +109,7 @@
     total_reads = packed.shape[1] * packed.shape[2]
     rows = packed.shape[0]
     packed = packed.reshape(rows, total_reads)
-    chunk = 512 if total_reads % 512 == 0 else total_reads
+    chunk = 1024 if total_reads % 1024 == 0 else total_reads
     end_value = my_end.astype(jnp.float32).reshape(1)
     hessian, border, tip_data = pl.pallas_call(
         assemble_kernel,

time: 197 us -> 196 us (level)
  starting transfers between devices: 124 us -> 15.3 us
  Pallas kernels: 13.4 us -> 108 us
  matrix products: 0 us -> 7.26 us
  other arithmetic: 19.4 us -> 24.7 us
    ppermute x4, starting transfers between devices: 114 us -> 5.37 us  [butterfly_sum(): x = x + lax.ppermute(x, axis, pairs)]
    pallas_call x0 -> x1, Pallas kernels: none -> 95.6 us  [eliminate(): pl.pallas_call(eliminate_kernel, out_shape=[jax.ShapeDtypeStruct((mesh_wi...]
    dot_general x0 -> x3, matrix products: none -> 7.26 us  [contract_rows(): lax.dot_general(left, right, (((0,), (0,)), ((), ())), preferred_element_...]
    add x0 -> x1, other arithmetic: none -> 2.67 us  [eliminate(): interior = hessian[1] + prior_diag]
    concatenate x0 -> x1, other arithmetic: none -> 2.6 us  [eliminate(): start = jnp.concatenate([interior, coupling_block, border[1].T], axis=1)]
where the time goes in v9:
time: 196 us; the launch traced here: 195 us
  Pallas kernels  108 us (55%)
  other arithmetic  24.7 us (13%)
  waiting for transfers between devices  20.6 us (11%)
  starting transfers between devices  15.3 us (8%)
  local copies, waits for them, and re-layouts  12.5 us (6%)
  matrix products  7.26 us (4%)
  between operations  5.9 us (3%)
    pallas_call x1, Pallas kernels, eliminate(): pl.pallas_call(eliminate_kernel, out_shape=[jax.ShapeDtypeStruct((mesh_wi...  95.6 us
    ppermute x4, waiting for transfers between devices, butterfly_sum(): x = x + lax.ppermute(x, axis, pairs)  20.6 us
    pallas_call x1, Pallas kernels, assemble(): pl.pallas_call(assemble_kernel, grid=(total_reads // chunk,), in_specs=[p...  12.7 us
    broadcast_in_dim x3, other arithmetic, local(): return (sep_block[None], fill[None], sep_border[None], tip)  8.38 us
    all_to_all x1, starting transfers between devices, local(): lax.all_to_all(packed, 'tm', split_axis=2, concat_axis=1, tiled=True)  7.39 us
    dot_general x3, matrix products, contract_rows(): lax.dot_general(left, right, (((0,), (0,)), ((), ())), preferred_element_...  7.26 us
    unnamed x71, local copies, waits for them, and re-layouts  7.11 us
    ppermute x4, starting transfers between devices, butterfly_sum(): x = x + lax.ppermute(x, axis, pairs)  5.37 us
  transfers between devices with their start and end apart: 7, of which 4 were waited for; matrix products, arithmetic and copies ran while one was open for 4% of the time, Pallas kernels for 0%

profile of v9, /device:TPU:0, one launch (start us, length us, event | category | flops | bytes accessed | tf_op | source)
XLA Modules:
  0.0 194.6 jit_solution(5777089470888801960)
XLA Ops:
  0.6 0.7 convert_element_type.28
  1.7 1.0 copy.84
  2.7 1.0 copy.85
  3.8 2.2 %fusion.17 = f32[1024,1,24]{2,1,0:T(1,128)S(1)} fusion(f32[16,1,1024]{0,1,2:T(1,128)S(1)} %copy.85, f32[4,1,1024]{0,1,2:T(1,128)S(1)} %copy.84, f32[4,1,1024]{0,1,2:T(1,128)S(1)} %copy.83), kind=kLoop, calls=%fused_computation.118 | loop fusion | flops 49152 | bytes 196608
  6.6 1.9 reduce
  8.5 1.0 reshape.57
  9.6 7.4 %all-to-all-start = ((f32[16,1,1536]{2,1,0:T(1,128)}), f32[16,1,1536]{2,1,0:T(1,128)S(1)}, u32[]{:S(2)}, u32[]{:S(2)}) async-start(f32[16,1,1536]{2,1,0:T(1,128)} %reshape.57), calls=%async_computation | async-start | bytes 196608 | tf_op jit(solution)/shard_map/all_to_all | solution.py:235
  20.8 3.4 %broadcast_multiply_fusion = (f32[768,768]{1,0:T(8,128)S(1)}, f32[768,768]{1,0:T(8,128)}) fusion(f32[768,768]{1,0:T(8,128)} %param.9, f32[]{:T(128)} %bitcast.9, f32[]{:T(128)} %bitcast.7), kind=kLoop, calls=%fused_computation.18 | loop fusion | flops 1179648 | bytes 7077896 | tf_op jit(solution)/shard_map/mul | solution.py:243
  26.8 0.9 reduce.1
  27.7 0.9 reshape.58
  28.9 12.7 %shard_map.93 = (f32[2,768,768]{2,1,0:T(8,128)}, f32[2,16,768]{2,1,0:T(8,128)S(1)}, f32[16,16]{1,0:T(8,128)S(1)}) custom-call(f32[1]{0:T(128)} %bitcast.4.end_ref, f32[24,1024]{1,0:T(8,128)S(1)} %bitcast.217), custom_call_target="tpu_custom_call" | custom-call | tf_op jit(solution)/shard_map/pallas_call | solution.py:114
  41.6 110.8 %conditional.1 = (f32[768,768]{1,0:T(8,128)}, f32[16,768]{1,0:T(8,128)S(1)}, f32[16,16]{1,0:T(8,128)S(1)}) conditional(s32[]{:T(128)} %convert_element_type.29, () %tuple.16, (f32[2,768,768]{2,1,0:T(8,128)}, f32[768,768]{1,0:T(8,128)}, f32[2,16,768]{2,1,0:T(8,128)S(1)}, f32[768,768]{1,0:T(8,128)S(1)}) %tuple.17), branch_computations={%region_1.2_spmd, %region_2.3_spmd} | conditional | flops 2845582080 | bytes 79942736 | solution.py:259
  42.0 2.7 %bitcast_add_fusion = f32[768,768]{1,0:T(8,128)S(1)} fusion(f32[768,768]{1,0:T(8,128)} %get-tuple-element.9, f32[2,768,768]{2,1,0:T(8,128)} %get-tuple-element.8), kind=kLoop, calls=%fused_computation.8 | loop fusion | flops 589824 | bytes 7077888 | tf_op jit(solution)/shard_map/cond/branch_1_fun/add | solution.py:204
  44.6 2.6 %pad_maximum_fusion.start_ref = f32[768,1552]{1,0:T(8,128)} fusion(f32[768,16]{1,0:T(8,128)S(1)} %slice_bitcast_fusion, f32[768,768]{1,0:T(8,128)S(1)} %get-tuple-element.10, f32[768,768]{1,0:T(8,128)S(1)} %bitcast_add_fusion), kind=kLoop, calls=%fused_computation | loop fusion | flops 2383872 | bytes 9535488 | tf_op jit(solution)/shard_map/cond/branch_1_fun/concatenate | solution.py:205
  47.2 95.6 %branch_1_fun.1 = (f32[768,1552]{1,0:T(8,128)}, f32[768,784]{1,0:T(8,128)}) custom-call(f32[768,1552]{1,0:T(8,128)} %pad_maximum_fusion.start_ref), custom_call_target="tpu_custom_call" | custom-call | tf_op jit(solution)/shard_map/cond/branch_1_fun/pallas_call | solution.py:207
  142.8 4.2 %fusion.2 = f32[784,784]{1,0:T(8,128)S(1)} fusion(f32[768,784]{1,0:T(8,128)} %get-tuple-element.13, f32[768,1552]{1,0:T(8,128)} %get-tuple-element.12), kind=kOutput, calls=%fused_computation.9 | convolution fusion | flops 947122176 | bytes 7963648 | tf_op jit(solution)/shard_map/cond/branch_1_fun/dot_general | solution.py:62
  147.7 1.5 fusion.5
  149.2 1.6 add_negate_fusion
  150.8 1.6 slice.222
  152.4 3.4 %select_bitcast_fusion = (f32[1,768,768]{2,1,0:T(8,128)}, f32[768,768]{1,0:T(8,128)S(1)}) fusion(f32[768,768]{1,0:T(8,128)} %get-tuple-element.26, f32[768,768]{1,0:T(8,128)S(1)} %get-tuple-element.48, pred[]{:T(512)} %bitcast.8, pred[]{:T(512)S(6)} %gt.3), kind=kLoop, calls=%fused_computation.16 | loop fusion | flops 1769472 | bytes 9437186 | tf_op jit(solution)/shard_map/broadcast_in_dim | solution.py:273
  156.1 1.3 collective-permute-start
  157.4 1.2 collective-permute-start.2
  158.6 2.5 %collective-permute-done.2 = f32[16,16]{1,0:T(8,128)S(1)} collective-permute-done((f32[16,16]{1,0:T(8,128)S(1)}, f32[16,16]{1,0:T(8,128)S(1)}, u32[]{:S(2)}, u32[]{:S(2)}) %collective-permute-start.2) | collective-permute-done | bytes 1056 | tf_op jit(solution)/shard_map/ppermute | solution.py:24
  161.1 1.9 collective-permute-start.3
  163.1 13.4 %collective-permute-done.3 = f32[16,16]{1,0:T(8,128)S(1)} collective-permute-done((f32[16,16]{1,0:T(8,128)S(1)}, f32[16,16]{1,0:T(8,128)S(1)}, u32[]{:S(2)}, u32[]{:S(2)}) %collective-permute-start.3) | collective-permute-done | bytes 1056 | tf_op jit(solution)/shard_map/ppermute | solution.py:24
  176.5 3.6 %collective-permute-done.4 = f32[16,16]{1,0:T(8,128)S(1)} collective-permute-done((f32[16,16]{1,0:T(8,128)S(1)}, f32[16,16]{1,0:T(8,128)S(1)}, u32[]{:S(2)}, u32[]{:S(2)}) %collective-permute-start.4) | collective-permute-done | bytes 1056 | tf_op jit(solution)/shard_map/ppermute | solution.py:24
  180.1 2.3 %collective-permute-start.5 = (f32[16,16]{1,0:T(8,128)S(1)}, f32[16,16]{1,0:T(8,128)S(1)}, u32[]{:S(2)}, u32[]{:S(2)}) collective-permute-start(f32[16,16]{1,0:T(8,128)S(1)} %add.57), channel_id=1, source_target_pairs={{0,8},{1,9},{2,10},{3,11},{4,12},{5,13},{6,14},{7,15},{8,0},{9,1},... | collective-permute-start | bytes 3080 | tf_op jit(solution)/shard_map/ppermute | solution.py:24
  182.4 1.3 collective-permute-start.1
  183.7 1.0 collective-permute-done.5
  184.7 1.2 select_add_fusion
  189.0 1.3 copy-done
  190.2 4.4 %fusion.8 = f32[1,768,768]{2,1,0:T(8,128)} fusion(f32[768,768]{1,0:T(8,128)S(1)} %fusion.9, f32[768,768]{1,0:T(8,128)} %get-tuple-element.26, f32[768,768]{1,0:T(8,128)S(1)} %copy-done, f32[2,768,768]{2,1,0:T(8,128)} %get-tuple-element.24), kind=kLoop, calls=%fused_computation.15 | loop fusion | flops 1769472 | bytes 11796480 | tf_op jit(solution)/shard_map/broadcast_in_dim | solution.py:273
  (103 shorter events, 6.9 us)
Async XLA Ops:
  2.7 14.2 %copy-start.3 = (f32[3]{0:T(128)S(1)}, f32[3]{0:T(128)}, u32[]{:S(2)}) copy-start(f32[3]{0:T(128)} %param.8) | copy-start | bytes 40
  9.6 17.3 %all-to-all-start = ((f32[16,1,1536]{2,1,0:T(1,128)}), f32[16,1,1536]{2,1,0:T(1,128)S(1)}, u32[]{:S(2)}, u32[]{:S(2)}) async-start(f32[16,1,1536]{2,1,0:T(1,128)} %reshape.57), calls=%async_computation | async-start | bytes 196608 | tf_op jit(solution)/shard_map/all_to_all | solution.py:235
  20.8 3.4 %copy-start.4 = (s32[16]{0:T(128)S(1)}, s32[16]{0:T(128)}, u32[]{:S(2)}) copy-start(s32[16]{0:T(128)} %param.10) | copy-start | bytes 196
  142.8 4.2 %copy-start.1 = (f32[768,784]{1,0:T(8,128)S(1)}, f32[768,784]{1,0:T(8,128)}, u32[]{:S(2)}) copy-start(f32[768,784]{1,0:T(8,128)} %get-tuple-element.13) | copy-start | bytes 7225348 | tf_op jit(solution)/shard_map/cond
  142.8 4.9 %copy-start.2 = (f32[768,1552]{1,0:T(8,128)S(1)}, f32[768,1552]{1,0:T(8,128)}, u32[]{:S(2)}) copy-start(f32[768,1552]{1,0:T(8,128)} %get-tuple-element.12) | copy-start | bytes 14303236 | tf_op jit(solution)/shard_map/cond
  156.1 30.4 %collective-permute-start = (f32[21,128,128]{2,1,0:T(8,128)S(1)}, f32[21,128,128]{2,1,0:T(8,128)S(1)}, u32[]{:S(2)}, u32[]{:S(2)}) collective-permute-start(f32[21,128,128]{2,1,0:T(8,128)S(1)} %constant_dynamic-update-slice_fusion), channel_id=1, source_target_pairs={{1,0},{2,1},{3,2},{4,3},{5,4},{6,5},{7,6},{8,7},{9,8},{10,9},{11,1... | collective-permute-start | bytes 4128776 | tf_op jit(solution)/shard_map/ppermute | solution.py:14
  157.4 3.7 %collective-permute-start.2 = (f32[16,16]{1,0:T(8,128)S(1)}, f32[16,16]{1,0:T(8,128)S(1)}, u32[]{:S(2)}, u32[]{:S(2)}) collective-permute-start(f32[16,16]{1,0:T(8,128)S(1)} %add.54), channel_id=1, source_target_pairs={{0,1},{1,0},{2,3},{3,2},{4,5},{5,4},{6,7},{7,6},{8,9},{9,8},{10,11... | collective-permute-start | bytes 3080 | tf_op jit(solution)/shard_map/ppermute | solution.py:24
  161.1 15.3 %collective-permute-start.3 = (f32[16,16]{1,0:T(8,128)S(1)}, f32[16,16]{1,0:T(8,128)S(1)}, u32[]{:S(2)}, u32[]{:S(2)}) collective-permute-start(f32[16,16]{1,0:T(8,128)S(1)} %add.55), channel_id=1, source_target_pairs={{0,2},{1,3},{2,0},{3,1},{4,6},{5,7},{6,4},{7,5},{8,10},{9,11},{10,... | collective-permute-start | bytes 3080 | tf_op jit(solution)/shard_map/ppermute | solution.py:24
  176.5 3.7 %collective-permute-start.4 = (f32[16,16]{1,0:T(8,128)S(1)}, f32[16,16]{1,0:T(8,128)S(1)}, u32[]{:S(2)}, u32[]{:S(2)}) collective-permute-start(f32[16,16]{1,0:T(8,128)S(1)} %add.56), channel_id=1, source_target_pairs={{0,4},{1,5},{2,6},{3,7},{4,0},{5,1},{6,2},{7,3},{8,12},{9,13},{10,... | collective-permute-start | bytes 3080 | tf_op jit(solution)/shard_map/ppermute | solution.py:24
  180.1 4.5 %collective-permute-start.5 = (f32[16,16]{1,0:T(8,128)S(1)}, f32[16,16]{1,0:T(8,128)S(1)}, u32[]{:S(2)}, u32[]{:S(2)}) collective-permute-start(f32[16,16]{1,0:T(8,128)S(1)} %add.57), channel_id=1, source_target_pairs={{0,8},{1,9},{2,10},{3,11},{4,12},{5,13},{6,14},{7,15},{8,0},{9,1},... | collective-permute-start | bytes 3080 | tf_op jit(solution)/shard_map/ppermute | solution.py:24
  182.4 3.5 %collective-permute-start.1 = (f32[16,768]{1,0:T(8,128)S(1)}, f32[16,768]{1,0:T(8,128)S(1)}, u32[]{:S(2)}, u32[]{:S(2)}) collective-permute-start(f32[16,768]{1,0:T(8,128)S(1)} %broadcast_select_fusion.1), channel_id=1, source_target_pairs={{1,0},{2,1},{3,2},{4,3},{5,4},{6,5},{7,6},{8,7},{9,8},{10,9},{11,1... | collective-permute-start | bytes 147464 | tf_op jit(solution)/shard_map/ppermute | solution.py:14
  188.6 1.7 copy-start

commit v10 on v9

--- a/solution.py
+++ b/solution.py
@@ -174,9 +174,9 @@
         inverse = 1.0 / pivot
         scaled_row = row * inverse
         update = current - col * scaled_row
-        update = jnp.where(sub == k, scaled_row, update)
+        fixed_row = jnp.where(lane_row == k, -inverse, scaled_row)
         update = jnp.where(lane == k, col * inverse, update)
-        update = jnp.where((sub == k) & (lane == k), -inverse, update)
+        update = jnp.where(sub == k, fixed_row, update)
         block_ref[...] = update
         return carry
 

time: 196 us -> 193 us (0.985)
  starting transfers between devices: 15.3 us -> 19.3 us
  waiting for transfers between devices: 20.6 us -> 16.6 us
  Pallas kernels: 108 us -> 105 us
    ppermute x4, waiting for transfers between devices: 20.6 us -> 16.3 us  [butterfly_sum(): x = x + lax.ppermute(x, axis, pairs)]
    ppermute x4, starting transfers between devices: 5.37 us -> 9.3 us  [butterfly_sum(): x = x + lax.ppermute(x, axis, pairs)]
    pallas_call x1, Pallas kernels: 95.6 us -> 92.2 us  [eliminate(): pl.pallas_call(eliminate_kernel, out_shape=[jax.ShapeDtypeStruct((mesh_wi...]
  transfers between devices with their start and end apart: 7 -> 7, of which waited for: 4 -> 5; matrix products, arithmetic and copies ran while one was open for 4% -> 4% of each run, Pallas kernels for 0% -> 0%
where the time goes in v10:
time: 193 us; the launch traced here: 191 us
  Pallas kernels  105 us (54%)
  other arithmetic  24.7 us (13%)
  starting transfers between devices  19.3 us (10%)
  waiting for transfers between devices  16.6 us (9%)
  local copies, waits for them, and re-layouts  12.5 us (6%)
  matrix products  7.26 us (4%)
  between operations  5.9 us (3%)
    pallas_call x1, Pallas kernels, eliminate(): pl.pallas_call(eliminate_kernel, out_shape=[jax.ShapeDtypeStruct((mesh_wi...  92.2 us
    ppermute x4, waiting for transfers between devices, butterfly_sum(): x = x + lax.ppermute(x, axis, pairs)  16.3 us
    pallas_call x1, Pallas kernels, assemble(): pl.pallas_call(assemble_kernel, grid=(total_reads // chunk,), in_specs=[p...  12.7 us
    ppermute x4, starting transfers between devices, butterfly_sum(): x = x + lax.ppermute(x, axis, pairs)  9.3 us
    broadcast_in_dim x3, other arithmetic, local(): return (sep_block[None], fill[None], sep_border[None], tip)  8.38 us
    all_to_all x1, starting transfers between devices, local(): lax.all_to_all(packed, 'tm', split_axis=2, concat_axis=1, tiled=True)  7.39 us
    dot_general x3, matrix products, contract_rows(): lax.dot_general(left, right, (((0,), (0,)), ((), ())), preferred_element_...  7.26 us
    unnamed x71, local copies, waits for them, and re-layouts  7.11 us
  transfers between devices with their start and end apart: 7, of which 5 were waited for; matrix products, arithmetic and copies ran while one was open for 4% of the time, Pallas kernels for 0%

profile of v10, /device:TPU:0, one launch (start us, length us, event | category | flops | bytes accessed | tf_op | source)
XLA Modules:
  0.0 191.1 jit_solution(5735198391434655602)
XLA Ops:
  0.6 0.7 convert_element_type.28
  1.7 1.0 copy.84
  2.7 1.0 copy.85
  3.8 2.2 %fusion.17 = f32[1024,1,24]{2,1,0:T(1,128)S(1)} fusion(f32[16,1,1024]{0,1,2:T(1,128)S(1)} %copy.85, f32[4,1,1024]{0,1,2:T(1,128)S(1)} %copy.84, f32[4,1,1024]{0,1,2:T(1,128)S(1)} %copy.83), kind=kLoop, calls=%fused_computation.118 | loop fusion | flops 49152 | bytes 196608
  6.6 1.9 %reduce = f32[1024,24]{1,0:T(8,128)S(1)} reduce(f32[1024,1,24]{2,1,0:T(1,128)S(1)} %fusion.17, f32[]{:T(128)} %broadcast.22), dimensions={1}, to_apply=%fusion.17.reduce_sub_computation | reduce | bytes 196612
  8.5 1.0 reshape.57
  9.6 7.4 %all-to-all-start = ((f32[16,1,1536]{2,1,0:T(1,128)}), f32[16,1,1536]{2,1,0:T(1,128)S(1)}, u32[]{:S(2)}, u32[]{:S(2)}) async-start(f32[16,1,1536]{2,1,0:T(1,128)} %reshape.57), calls=%async_computation | async-start | bytes 196608 | tf_op jit(solution)/shard_map/all_to_all | solution.py:235
  20.8 3.4 %broadcast_multiply_fusion = (f32[768,768]{1,0:T(8,128)S(1)}, f32[768,768]{1,0:T(8,128)}) fusion(f32[768,768]{1,0:T(8,128)} %param.9, f32[]{:T(128)} %bitcast.9, f32[]{:T(128)} %bitcast.7), kind=kLoop, calls=%fused_computation.18 | loop fusion | flops 1179648 | bytes 7077896 | tf_op jit(solution)/shard_map/mul | solution.py:243
  26.8 0.9 reduce.1
  27.7 0.9 reshape.58
  28.9 12.7 %shard_map.93 = (f32[2,768,768]{2,1,0:T(8,128)}, f32[2,16,768]{2,1,0:T(8,128)S(1)}, f32[16,16]{1,0:T(8,128)S(1)}) custom-call(f32[1]{0:T(128)} %bitcast.4.end_ref, f32[24,1024]{1,0:T(8,128)S(1)} %bitcast.217), custom_call_target="tpu_custom_call" | custom-call | tf_op jit(solution)/shard_map/pallas_call | solution.py:114
  41.6 107.4 %conditional.1 = (f32[768,768]{1,0:T(8,128)}, f32[16,768]{1,0:T(8,128)S(1)}, f32[16,16]{1,0:T(8,128)S(1)}) conditional(s32[]{:T(128)} %convert_element_type.29, () %tuple.16, (f32[2,768,768]{2,1,0:T(8,128)}, f32[768,768]{1,0:T(8,128)}, f32[2,16,768]{2,1,0:T(8,128)S(1)}, f32[768,768]{1,0:T(8,128)S(1)}) %tuple.17), branch_computations={%region_1.2_spmd, %region_2.3_spmd} | conditional | flops 2845582080 | bytes 79942736 | solution.py:259
  42.0 2.7 %bitcast_add_fusion = f32[768,768]{1,0:T(8,128)S(1)} fusion(f32[768,768]{1,0:T(8,128)} %get-tuple-element.9, f32[2,768,768]{2,1,0:T(8,128)} %get-tuple-element.8), kind=kLoop, calls=%fused_computation.8 | loop fusion | flops 589824 | bytes 7077888 | tf_op jit(solution)/shard_map/cond/branch_1_fun/add | solution.py:204
  44.6 2.6 %pad_maximum_fusion.start_ref = f32[768,1552]{1,0:T(8,128)} fusion(f32[768,16]{1,0:T(8,128)S(1)} %slice_bitcast_fusion, f32[768,768]{1,0:T(8,128)S(1)} %get-tuple-element.10, f32[768,768]{1,0:T(8,128)S(1)} %bitcast_add_fusion), kind=kLoop, calls=%fused_computation | loop fusion | flops 2383872 | bytes 9535488 | tf_op jit(solution)/shard_map/cond/branch_1_fun/concatenate | solution.py:205
  47.2 92.2 %branch_1_fun.1 = (f32[768,1552]{1,0:T(8,128)}, f32[768,784]{1,0:T(8,128)}) custom-call(f32[768,1552]{1,0:T(8,128)} %pad_maximum_fusion.start_ref), custom_call_target="tpu_custom_call" | custom-call | tf_op jit(solution)/shard_map/cond/branch_1_fun/pallas_call | solution.py:207
  139.4 4.2 %fusion.2 = f32[784,784]{1,0:T(8,128)S(1)} fusion(f32[768,784]{1,0:T(8,128)} %get-tuple-element.13, f32[768,1552]{1,0:T(8,128)} %get-tuple-element.12), kind=kOutput, calls=%fused_computation.9 | convolution fusion | flops 947122176 | bytes 7963648 | tf_op jit(solution)/shard_map/cond/branch_1_fun/dot_general | solution.py:62
  143.6 0.7 copy-done.2
  144.3 1.5 fusion.5
  145.8 1.6 add_negate_fusion
  147.4 1.6 slice.222
  149.0 3.4 %select_bitcast_fusion = (f32[1,768,768]{2,1,0:T(8,128)}, f32[768,768]{1,0:T(8,128)S(1)}) fusion(f32[768,768]{1,0:T(8,128)} %get-tuple-element.26, f32[768,768]{1,0:T(8,128)S(1)} %get-tuple-element.48, pred[]{:T(512)} %bitcast.8, pred[]{:T(512)S(6)} %gt.3), kind=kLoop, calls=%fused_computation.16 | loop fusion | flops 1769472 | bytes 9437186 | tf_op jit(solution)/shard_map/broadcast_in_dim | solution.py:273
  152.7 1.3 collective-permute-start
  154.0 1.2 collective-permute-start.2
  155.2 2.5 %collective-permute-done.2 = f32[16,16]{1,0:T(8,128)S(1)} collective-permute-done((f32[16,16]{1,0:T(8,128)S(1)}, f32[16,16]{1,0:T(8,128)S(1)}, u32[]{:S(2)}, u32[]{:S(2)}) %collective-permute-start.2) | collective-permute-done | bytes 1056 | tf_op jit(solution)/shard_map/ppermute | solution.py:24
  157.7 3.6 %collective-permute-done.3 = f32[16,16]{1,0:T(8,128)S(1)} collective-permute-done((f32[16,16]{1,0:T(8,128)S(1)}, f32[16,16]{1,0:T(8,128)S(1)}, u32[]{:S(2)}, u32[]{:S(2)}) %collective-permute-start.3) | collective-permute-done | bytes 1056 | tf_op jit(solution)/shard_map/ppermute | solution.py:24
  161.4 1.9 %collective-permute-start.4 = (f32[16,16]{1,0:T(8,128)S(1)}, f32[16,16]{1,0:T(8,128)S(1)}, u32[]{:S(2)}, u32[]{:S(2)}) collective-permute-start(f32[16,16]{1,0:T(8,128)S(1)} %add.56), channel_id=1, source_target_pairs={{0,4},{1,5},{2,6},{3,7},{4,0},{5,1},{6,2},{7,3},{8,12},{9,13},{10,... | collective-permute-start | bytes 3080 | tf_op jit(solution)/shard_map/ppermute | solution.py:24
  163.3 9.8 %collective-permute-done.4 = f32[16,16]{1,0:T(8,128)S(1)} collective-permute-done((f32[16,16]{1,0:T(8,128)S(1)}, f32[16,16]{1,0:T(8,128)S(1)}, u32[]{:S(2)}, u32[]{:S(2)}) %collective-permute-start.4) | collective-permute-done | bytes 1056 | tf_op jit(solution)/shard_map/ppermute | solution.py:24
  173.1 6.2 %collective-permute-start.5 = (f32[16,16]{1,0:T(8,128)S(1)}, f32[16,16]{1,0:T(8,128)S(1)}, u32[]{:S(2)}, u32[]{:S(2)}) collective-permute-start(f32[16,16]{1,0:T(8,128)S(1)} %add.57), channel_id=1, source_target_pairs={{0,8},{1,9},{2,10},{3,11},{4,12},{5,13},{6,14},{7,15},{8,0},{9,1},... | collective-permute-start | bytes 3080 | tf_op jit(solution)/shard_map/ppermute | solution.py:24
  179.3 1.3 collective-permute-start.1
  180.9 1.2 select_add_fusion
  185.5 1.3 copy-done
  186.7 4.4 %fusion.8 = f32[1,768,768]{2,1,0:T(8,128)} fusion(f32[768,768]{1,0:T(8,128)S(1)} %fusion.9, f32[768,768]{1,0:T(8,128)} %get-tuple-element.26, f32[768,768]{1,0:T(8,128)S(1)} %copy-done, f32[2,768,768]{2,1,0:T(8,128)} %get-tuple-element.24), kind=kLoop, calls=%fused_computation.15 | loop fusion | flops 1769472 | bytes 11796480 | tf_op jit(solution)/shard_map/broadcast_in_dim | solution.py:273
  (103 shorter events, 6.8 us)
Async XLA Ops:
  2.7 14.2 %copy-start.3 = (f32[3]{0:T(128)S(1)}, f32[3]{0:T(128)}, u32[]{:S(2)}) copy-start(f32[3]{0:T(128)} %param.8) | copy-start | bytes 40
  9.6 17.3 %all-to-all-start = ((f32[16,1,1536]{2,1,0:T(1,128)}), f32[16,1,1536]{2,1,0:T(1,128)S(1)}, u32[]{:S(2)}, u32[]{:S(2)}) async-start(f32[16,1,1536]{2,1,0:T(1,128)} %reshape.57), calls=%async_computation | async-start | bytes 196608 | tf_op jit(solution)/shard_map/all_to_all | solution.py:235
  20.8 3.4 %copy-start.4 = (s32[16]{0:T(128)S(1)}, s32[16]{0:T(128)}, u32[]{:S(2)}) copy-start(s32[16]{0:T(128)} %param.10) | copy-start | bytes 196
  139.4 4.2 %copy-start.1 = (f32[768,784]{1,0:T(8,128)S(1)}, f32[768,784]{1,0:T(8,128)}, u32[]{:S(2)}) copy-start(f32[768,784]{1,0:T(8,128)} %get-tuple-element.13) | copy-start | bytes 7225348 | tf_op jit(solution)/shard_map/cond
  139.4 4.9 %copy-start.2 = (f32[768,1552]{1,0:T(8,128)S(1)}, f32[768,1552]{1,0:T(8,128)}, u32[]{:S(2)}) copy-start(f32[768,1552]{1,0:T(8,128)} %get-tuple-element.12) | copy-start | bytes 14303236 | tf_op jit(solution)/shard_map/cond
  152.7 30.4 %collective-permute-start = (f32[21,128,128]{2,1,0:T(8,128)S(1)}, f32[21,128,128]{2,1,0:T(8,128)S(1)}, u32[]{:S(2)}, u32[]{:S(2)}) collective-permute-start(f32[21,128,128]{2,1,0:T(8,128)S(1)} %constant_dynamic-update-slice_fusion), channel_id=1, source_target_pairs={{1,0},{2,1},{3,2},{4,3},{5,4},{6,5},{7,6},{8,7},{9,8},{10,9},{11,1... | collective-permute-start | bytes 4128776 | tf_op jit(solution)/shard_map/ppermute | solution.py:14
  154.0 3.7 %collective-permute-start.2 = (f32[16,16]{1,0:T(8,128)S(1)}, f32[16,16]{1,0:T(8,128)S(1)}, u32[]{:S(2)}, u32[]{:S(2)}) collective-permute-start(f32[16,16]{1,0:T(8,128)S(1)} %add.54), channel_id=1, source_target_pairs={{0,1},{1,0},{2,3},{3,2},{4,5},{5,4},{6,7},{7,6},{8,9},{9,8},{10,11... | collective-permute-start | bytes 3080 | tf_op jit(solution)/shard_map/ppermute | solution.py:24
  157.7 3.7 %collective-permute-start.3 = (f32[16,16]{1,0:T(8,128)S(1)}, f32[16,16]{1,0:T(8,128)S(1)}, u32[]{:S(2)}, u32[]{:S(2)}) collective-permute-start(f32[16,16]{1,0:T(8,128)S(1)} %add.55), channel_id=1, source_target_pairs={{0,2},{1,3},{2,0},{3,1},{4,6},{5,7},{6,4},{7,5},{8,10},{9,11},{10,... | collective-permute-start | bytes 3080 | tf_op jit(solution)/shard_map/ppermute | solution.py:24
  161.4 11.7 %collective-permute-start.4 = (f32[16,16]{1,0:T(8,128)S(1)}, f32[16,16]{1,0:T(8,128)S(1)}, u32[]{:S(2)}, u32[]{:S(2)}) collective-permute-start(f32[16,16]{1,0:T(8,128)S(1)} %add.56), channel_id=1, source_target_pairs={{0,4},{1,5},{2,6},{3,7},{4,0},{5,1},{6,2},{7,3},{8,12},{9,13},{10,... | collective-permute-start | bytes 3080 | tf_op jit(solution)/shard_map/ppermute | solution.py:24
  173.1 7.8 %collective-permute-start.5 = (f32[16,16]{1,0:T(8,128)S(1)}, f32[16,16]{1,0:T(8,128)S(1)}, u32[]{:S(2)}, u32[]{:S(2)}) collective-permute-start(f32[16,16]{1,0:T(8,128)S(1)} %add.57), channel_id=1, source_target_pairs={{0,8},{1,9},{2,10},{3,11},{4,12},{5,13},{6,14},{7,15},{8,0},{9,1},... | collective-permute-start | bytes 3080 | tf_op jit(solution)/shard_map/ppermute | solution.py:24
  179.3 3.1 %collective-permute-start.1 = (f32[16,768]{1,0:T(8,128)S(1)}, f32[16,768]{1,0:T(8,128)S(1)}, u32[]{:S(2)}, u32[]{:S(2)}) collective-permute-start(f32[16,768]{1,0:T(8,128)S(1)} %broadcast_select_fusion.1), channel_id=1, source_target_pairs={{1,0},{2,1},{3,2},{4,3},{5,4},{6,5},{7,6},{8,7},{9,8},{10,9},{11,1... | collective-permute-start | bytes 147464 | tf_op jit(solution)/shard_map/ppermute | solution.py:14
  185.1 1.7 copy-start

commit v11 on v10

--- a/solution.py
+++ b/solution.py
@@ -180,7 +180,7 @@
         block_ref[...] = update
         return carry
 
-    lax.fori_loop(0, size, body, 0)
+    lax.fori_loop(0, size, body, 0, unroll=2)
 
 
 def eliminate_kernel(start_ref, work_ref, solved_ref, block_ref):

time: 193 us -> 193 us (level)
    ppermute x4, waiting for transfers between devices: 16.3 us -> 18.3 us  [butterfly_sum(): x = x + lax.ppermute(x, axis, pairs)]
  transfers between devices with their start and end apart: 7 -> 7, of which waited for: 5 -> 4; matrix products, arithmetic and copies ran while one was open for 4% -> 4% of each run, Pallas kernels for 0% -> 0%
where the time goes in v11:
time: 193 us; the launch traced here: 191 us
  Pallas kernels  105 us (54%)
  other arithmetic  24.7 us (13%)
  waiting for transfers between devices  18.3 us (9%)
  starting transfers between devices  17.5 us (9%)
  local copies, waits for them, and re-layouts  12.5 us (6%)
  matrix products  7.26 us (4%)
  between operations  5.9 us (3%)
    pallas_call x1, Pallas kernels, eliminate(): pl.pallas_call(eliminate_kernel, out_shape=[jax.ShapeDtypeStruct((mesh_wi...  92.4 us
    ppermute x4, waiting for transfers between devices, butterfly_sum(): x = x + lax.ppermute(x, axis, pairs)  18.3 us
    pallas_call x1, Pallas kernels, assemble(): pl.pallas_call(assemble_kernel, grid=(total_reads // chunk,), in_specs=[p...  12.7 us
    broadcast_in_dim x3, other arithmetic, local(): return (sep_block[None], fill[None], sep_border[None], tip)  8.38 us
    ppermute x4, starting transfers between devices, butterfly_sum(): x = x + lax.ppermute(x, axis, pairs)  7.56 us
    all_to_all x1, starting transfers between devices, local(): lax.all_to_all(packed, 'tm', split_axis=2, concat_axis=1, tiled=True)  7.39 us
    dot_general x3, matrix products, contract_rows(): lax.dot_general(left, right, (((0,), (0,)), ((), ())), preferred_element_...  7.26 us
    unnamed x71, local copies, waits for them, and re-layouts  7.11 us
  transfers between devices with their start and end apart: 7, of which 4 were waited for; matrix products, arithmetic and copies ran while one was open for 4% of the time, Pallas kernels for 0%

profile of v11, /device:TPU:0, one launch (start us, length us, event | category | flops | bytes accessed | tf_op | source)
XLA Modules:
  0.0 191.4 jit_solution(4540972230590992327)
XLA Ops:
  0.6 0.7 convert_element_type.28
  1.7 1.0 copy.84
  2.7 1.0 copy.85
  3.8 2.2 %fusion.17 = f32[1024,1,24]{2,1,0:T(1,128)S(1)} fusion(f32[16,1,1024]{0,1,2:T(1,128)S(1)} %copy.85, f32[4,1,1024]{0,1,2:T(1,128)S(1)} %copy.84, f32[4,1,1024]{0,1,2:T(1,128)S(1)} %copy.83), kind=kLoop, calls=%fused_computation.118 | loop fusion | flops 49152 | bytes 196608
  6.6 1.9 %reduce = f32[1024,24]{1,0:T(8,128)S(1)} reduce(f32[1024,1,24]{2,1,0:T(1,128)S(1)} %fusion.17, f32[]{:T(128)} %broadcast.22), dimensions={1}, to_apply=%fusion.17.reduce_sub_computation | reduce | bytes 196612
  8.5 1.0 reshape.57
  9.6 7.4 %all-to-all-start = ((f32[16,1,1536]{2,1,0:T(1,128)}), f32[16,1,1536]{2,1,0:T(1,128)S(1)}, u32[]{:S(2)}, u32[]{:S(2)}) async-start(f32[16,1,1536]{2,1,0:T(1,128)} %reshape.57), calls=%async_computation | async-start | bytes 196608 | tf_op jit(solution)/shard_map/all_to_all | solution.py:235
  20.8 3.4 %broadcast_multiply_fusion = (f32[768,768]{1,0:T(8,128)S(1)}, f32[768,768]{1,0:T(8,128)}) fusion(f32[768,768]{1,0:T(8,128)} %param.9, f32[]{:T(128)} %bitcast.9, f32[]{:T(128)} %bitcast.7), kind=kLoop, calls=%fused_computation.18 | loop fusion | flops 1179648 | bytes 7077896 | tf_op jit(solution)/shard_map/mul | solution.py:243
  26.8 0.9 reduce.1
  27.7 0.9 reshape.58
  28.9 12.7 %shard_map.93 = (f32[2,768,768]{2,1,0:T(8,128)}, f32[2,16,768]{2,1,0:T(8,128)S(1)}, f32[16,16]{1,0:T(8,128)S(1)}) custom-call(f32[1]{0:T(128)} %bitcast.4.end_ref, f32[24,1024]{1,0:T(8,128)S(1)} %bitcast.217), custom_call_target="tpu_custom_call" | custom-call | tf_op jit(solution)/shard_map/pallas_call | solution.py:114
  41.6 107.6 %conditional.1 = (f32[768,768]{1,0:T(8,128)}, f32[16,768]{1,0:T(8,128)S(1)}, f32[16,16]{1,0:T(8,128)S(1)}) conditional(s32[]{:T(128)} %convert_element_type.29, () %tuple.16, (f32[2,768,768]{2,1,0:T(8,128)}, f32[768,768]{1,0:T(8,128)}, f32[2,16,768]{2,1,0:T(8,128)S(1)}, f32[768,768]{1,0:T(8,128)S(1)}) %tuple.17), branch_computations={%region_1.2_spmd, %region_2.3_spmd} | conditional | flops 2845582080 | bytes 79942736 | solution.py:259
  42.0 2.7 %bitcast_add_fusion = f32[768,768]{1,0:T(8,128)S(1)} fusion(f32[768,768]{1,0:T(8,128)} %get-tuple-element.9, f32[2,768,768]{2,1,0:T(8,128)} %get-tuple-element.8), kind=kLoop, calls=%fused_computation.8 | loop fusion | flops 589824 | bytes 7077888 | tf_op jit(solution)/shard_map/cond/branch_1_fun/add | solution.py:204
  44.6 2.6 %pad_maximum_fusion.start_ref = f32[768,1552]{1,0:T(8,128)} fusion(f32[768,16]{1,0:T(8,128)S(1)} %slice_bitcast_fusion, f32[768,768]{1,0:T(8,128)S(1)} %get-tuple-element.10, f32[768,768]{1,0:T(8,128)S(1)} %bitcast_add_fusion), kind=kLoop, calls=%fused_computation | loop fusion | flops 2383872 | bytes 9535488 | tf_op jit(solution)/shard_map/cond/branch_1_fun/concatenate | solution.py:205
  47.2 92.4 %branch_1_fun.1 = (f32[768,1552]{1,0:T(8,128)}, f32[768,784]{1,0:T(8,128)}) custom-call(f32[768,1552]{1,0:T(8,128)} %pad_maximum_fusion.start_ref), custom_call_target="tpu_custom_call" | custom-call | tf_op jit(solution)/shard_map/cond/branch_1_fun/pallas_call | solution.py:207
  139.7 4.2 %fusion.2 = f32[784,784]{1,0:T(8,128)S(1)} fusion(f32[768,784]{1,0:T(8,128)} %get-tuple-element.13, f32[768,1552]{1,0:T(8,128)} %get-tuple-element.12), kind=kOutput, calls=%fused_computation.9 | convolution fusion | flops 947122176 | bytes 7963648 | tf_op jit(solution)/shard_map/cond/branch_1_fun/dot_general | solution.py:62
  144.6 1.5 fusion.5
  146.0 1.6 add_negate_fusion
  147.7 1.6 slice.222
  149.3 3.4 %select_bitcast_fusion = (f32[1,768,768]{2,1,0:T(8,128)}, f32[768,768]{1,0:T(8,128)S(1)}) fusion(f32[768,768]{1,0:T(8,128)} %get-tuple-element.26, f32[768,768]{1,0:T(8,128)S(1)} %get-tuple-element.48, pred[]{:T(512)} %bitcast.8, pred[]{:T(512)S(6)} %gt.3), kind=kLoop, calls=%fused_computation.16 | loop fusion | flops 1769472 | bytes 9437186 | tf_op jit(solution)/shard_map/broadcast_in_dim | solution.py:273
  153.0 1.3 collective-permute-start
  154.3 1.2 collective-permute-start.2
  155.5 2.5 %collective-permute-done.2 = f32[16,16]{1,0:T(8,128)S(1)} collective-permute-done((f32[16,16]{1,0:T(8,128)S(1)}, f32[16,16]{1,0:T(8,128)S(1)}, u32[]{:S(2)}, u32[]{:S(2)}) %collective-permute-start.2) | collective-permute-done | bytes 1056 | tf_op jit(solution)/shard_map/ppermute | solution.py:24
  158.0 1.9 %collective-permute-start.3 = (f32[16,16]{1,0:T(8,128)S(1)}, f32[16,16]{1,0:T(8,128)S(1)}, u32[]{:S(2)}, u32[]{:S(2)}) collective-permute-start(f32[16,16]{1,0:T(8,128)S(1)} %add.55), channel_id=1, source_target_pairs={{0,2},{1,3},{2,0},{3,1},{4,6},{5,7},{6,4},{7,5},{8,10},{9,11},{10,... | collective-permute-start | bytes 3080 | tf_op jit(solution)/shard_map/ppermute | solution.py:24
  159.9 13.3 %collective-permute-done.3 = f32[16,16]{1,0:T(8,128)S(1)} collective-permute-done((f32[16,16]{1,0:T(8,128)S(1)}, f32[16,16]{1,0:T(8,128)S(1)}, u32[]{:S(2)}, u32[]{:S(2)}) %collective-permute-start.3) | collective-permute-done | bytes 1056 | tf_op jit(solution)/shard_map/ppermute | solution.py:24
  173.2 1.8 collective-permute-start.4
  175.0 1.9 collective-permute-done.4
  176.9 2.7 %collective-permute-start.5 = (f32[16,16]{1,0:T(8,128)S(1)}, f32[16,16]{1,0:T(8,128)S(1)}, u32[]{:S(2)}, u32[]{:S(2)}) collective-permute-start(f32[16,16]{1,0:T(8,128)S(1)} %add.57), channel_id=1, source_target_pairs={{0,8},{1,9},{2,10},{3,11},{4,12},{5,13},{6,14},{7,15},{8,0},{9,1},... | collective-permute-start | bytes 3080 | tf_op jit(solution)/shard_map/ppermute | solution.py:24
  179.6 1.3 collective-permute-start.1
  181.4 1.2 select_add_fusion
  185.7 1.3 copy-done
  187.0 4.4 %fusion.8 = f32[1,768,768]{2,1,0:T(8,128)} fusion(f32[768,768]{1,0:T(8,128)S(1)} %fusion.9, f32[768,768]{1,0:T(8,128)} %get-tuple-element.26, f32[768,768]{1,0:T(8,128)S(1)} %copy-done, f32[2,768,768]{2,1,0:T(8,128)} %get-tuple-element.24), kind=kLoop, calls=%fused_computation.15 | loop fusion | flops 1769472 | bytes 11796480 | tf_op jit(solution)/shard_map/broadcast_in_dim | solution.py:273
  (103 shorter events, 7.5 us)
Async XLA Ops:
  2.7 14.2 %copy-start.3 = (f32[3]{0:T(128)S(1)}, f32[3]{0:T(128)}, u32[]{:S(2)}) copy-start(f32[3]{0:T(128)} %param.8) | copy-start | bytes 40
  9.6 17.3 %all-to-all-start = ((f32[16,1,1536]{2,1,0:T(1,128)}), f32[16,1,1536]{2,1,0:T(1,128)S(1)}, u32[]{:S(2)}, u32[]{:S(2)}) async-start(f32[16,1,1536]{2,1,0:T(1,128)} %reshape.57), calls=%async_computation | async-start | bytes 196608 | tf_op jit(solution)/shard_map/all_to_all | solution.py:235
  20.8 3.4 %copy-start.4 = (s32[16]{0:T(128)S(1)}, s32[16]{0:T(128)}, u32[]{:S(2)}) copy-start(s32[16]{0:T(128)} %param.10) | copy-start | bytes 196
  139.6 4.2 %copy-start.1 = (f32[768,784]{1,0:T(8,128)S(1)}, f32[768,784]{1,0:T(8,128)}, u32[]{:S(2)}) copy-start(f32[768,784]{1,0:T(8,128)} %get-tuple-element.13) | copy-start | bytes 7225348 | tf_op jit(solution)/shard_map/cond
  139.7 4.9 %copy-start.2 = (f32[768,1552]{1,0:T(8,128)S(1)}, f32[768,1552]{1,0:T(8,128)}, u32[]{:S(2)}) copy-start(f32[768,1552]{1,0:T(8,128)} %get-tuple-element.12) | copy-start | bytes 14303236 | tf_op jit(solution)/shard_map/cond
  153.0 30.4 %collective-permute-start = (f32[21,128,128]{2,1,0:T(8,128)S(1)}, f32[21,128,128]{2,1,0:T(8,128)S(1)}, u32[]{:S(2)}, u32[]{:S(2)}) collective-permute-start(f32[21,128,128]{2,1,0:T(8,128)S(1)} %constant_dynamic-update-slice_fusion), channel_id=1, source_target_pairs={{1,0},{2,1},{3,2},{4,3},{5,4},{6,5},{7,6},{8,7},{9,8},{10,9},{11,1... | collective-permute-start | bytes 4128776 | tf_op jit(solution)/shard_map/ppermute | solution.py:14
  154.3 3.7 %collective-permute-start.2 = (f32[16,16]{1,0:T(8,128)S(1)}, f32[16,16]{1,0:T(8,128)S(1)}, u32[]{:S(2)}, u32[]{:S(2)}) collective-permute-start(f32[16,16]{1,0:T(8,128)S(1)} %add.54), channel_id=1, source_target_pairs={{0,1},{1,0},{2,3},{3,2},{4,5},{5,4},{6,7},{7,6},{8,9},{9,8},{10,11... | collective-permute-start | bytes 3080 | tf_op jit(solution)/shard_map/ppermute | solution.py:24
  158.0 15.2 %collective-permute-start.3 = (f32[16,16]{1,0:T(8,128)S(1)}, f32[16,16]{1,0:T(8,128)S(1)}, u32[]{:S(2)}, u32[]{:S(2)}) collective-permute-start(f32[16,16]{1,0:T(8,128)S(1)} %add.55), channel_id=1, source_target_pairs={{0,2},{1,3},{2,0},{3,1},{4,6},{5,7},{6,4},{7,5},{8,10},{9,11},{10,... | collective-permute-start | bytes 3080 | tf_op jit(solution)/shard_map/ppermute | solution.py:24
  173.2 3.7 %collective-permute-start.4 = (f32[16,16]{1,0:T(8,128)S(1)}, f32[16,16]{1,0:T(8,128)S(1)}, u32[]{:S(2)}, u32[]{:S(2)}) collective-permute-start(f32[16,16]{1,0:T(8,128)S(1)} %add.56), channel_id=1, source_target_pairs={{0,4},{1,5},{2,6},{3,7},{4,0},{5,1},{6,2},{7,3},{8,12},{9,13},{10,... | collective-permute-start | bytes 3080 | tf_op jit(solution)/shard_map/ppermute | solution.py:24
  176.9 4.5 %collective-permute-start.5 = (f32[16,16]{1,0:T(8,128)S(1)}, f32[16,16]{1,0:T(8,128)S(1)}, u32[]{:S(2)}, u32[]{:S(2)}) collective-permute-start(f32[16,16]{1,0:T(8,128)S(1)} %add.57), channel_id=1, source_target_pairs={{0,8},{1,9},{2,10},{3,11},{4,12},{5,13},{6,14},{7,15},{8,0},{9,1},... | collective-permute-start | bytes 3080 | tf_op jit(solution)/shard_map/ppermute | solution.py:24
  179.6 3.1 %collective-permute-start.1 = (f32[16,768]{1,0:T(8,128)S(1)}, f32[16,768]{1,0:T(8,128)S(1)}, u32[]{:S(2)}, u32[]{:S(2)}) collective-permute-start(f32[16,768]{1,0:T(8,128)S(1)} %broadcast_select_fusion.1), channel_id=1, source_target_pairs={{1,0},{2,1},{3,2},{4,3},{5,4},{6,5},{7,6},{8,7},{9,8},{10,9},{11,1... | collective-permute-start | bytes 147464 | tf_op jit(solution)/shard_map/ppermute | solution.py:14
  185.3 1.7 copy-start
